TPU v7x, 512 devices: a whole 4x4x16 slice. The times are simulated.
512 devices in a mesh: section: 8 (over z_hi, core), tp: 64 (over x, z_lo, y).
Axes of the slice: x: 4, y: 4, z: 16 (z_hi: 4, z_lo: 4; z = z_hi * 4 + z_lo), core: 2. Of those that a mesh axis runs over, the one named last changes fastest.
Arguments:
- incoming: bfloat16 [8, 320, 8192], P('section', None, 'tp'), may hold values from -6 to 6
- norm_gain: bfloat16 [8, 8192], P('section', 'tp'), may hold values from 0.5 to 1.5
- query_weight: bfloat16 [8, 8192, 8192], P('section', 'tp'), may hold values from -0.0625 to 0.0625
- query_scale: float32 [8, 64, 64], P('section', 'tp'), may hold values from 0.3 to 3
- query_keep: int32 [8, 64, 64], P('section', 'tp'), may hold values from 0 to 1, as said below
- kv_weight: bfloat16 [8, 8192, 2048], P('section', 'tp'), may hold values from -0.0625 to 0.0625
- kv_scale: float32 [8, 64, 16], P('section', 'tp'), may hold values from 0.3 to 3
- kv_keep: int32 [8, 64, 16], P('section', 'tp'), may hold values from 0 to 1, as said below
- out_weight: bfloat16 [8, 8192, 8192], P('section', 'tp'), may hold values from -0.0625 to 0.0625
- out_scale: float32 [8, 64, 64], P('section', 'tp'), may hold values from 0.3 to 3
- out_keep: int32 [8, 64, 64], P('section', 'tp'), may hold values from 0 to 1, as said below
- documents: int32 [320], replicated, may hold values from 0 to 3, never falling along the last dimension, each value on 1 to 160 neighbouring positions
Outputs:
- passed: bfloat16 [8, 320, 8192], P('section', None, 'tp')
Inputs may be any that keep to these rules, and one draw needn't show every extreme that they name: `documents`: document numbers never fall along the tokens; every document has 1 to 160 tokens and one has exactly 160. `query_keep`: 1 keeps the block, 0 removes it. `kv_keep`: 1 keeps the block, 0 removes it. `out_keep`: 1 keeps the block, 0 removes it.
All inputs are finite; a program needn't handle non-finite values.
Results may differ from a plain program's by a relative error of at most 0.006.
Values may be sent and summed in bfloat16 or wider, within the bound.
No kernel may reach another device: no remote copies, remote signals or barrier semaphores. Data moves between devices by JAX's collectives and lax.ppermute only.
A program may use at most 64 MiB of HBM per device.

v0:
```python
import jax
import jax.numpy as jnp
from jax import lax
from jax.sharding import PartitionSpec as P

D = 8192
HEADS = 64
KV_HEADS = 8
HD = 128
BLK = 128


rope_base = 500000.0
epsilon = 1e-05


def passed_along(value, axis, steps):
    count = lax.axis_size(axis)
    pairs = [(source, (source + steps) % count) for source in range(count)]
    return lax.ppermute(value, axis, pairs)


def dequant(weight, scale, keep):
    row_count, col_count = weight.shape
    factor = scale * keep.astype(jnp.float32)
    blocks = weight.astype(jnp.float32).reshape(row_count // BLK, BLK, col_count // BLK, BLK)
    blocks = blocks * factor[:, None, :, None]
    return blocks.reshape(row_count, col_count).astype(jnp.bfloat16)


def rotate(values, first_col):
    row_count, col_count = values.shape
    columns = first_col + 2 * jnp.arange(col_count // 2, dtype=jnp.int32)
    frequency = rope_base ** (-(columns % HD).astype(jnp.float32) / HD)
    angles = jnp.arange(row_count, dtype=jnp.float32)[:, None] * frequency[None, :]
    paired = values.reshape(row_count, col_count // 2, 2)
    even_part = paired[:, :, 0]
    odd_part = paired[:, :, 1]
    cosine = jnp.cos(angles)
    sine = jnp.sin(angles)
    turned = jnp.stack(
        (even_part * cosine - odd_part * sine, even_part * sine + odd_part * cosine), axis=-1
    )
    return turned.reshape(row_count, col_count)


def rotate_keys(values, first_col, kv_width):
    col_ids = first_col + jnp.arange(values.shape[1], dtype=jnp.int32)
    return jnp.where(col_ids[None, :] < kv_width, rotate(values, first_col), values)


def local(
    incoming,
    norm_gain,
    query_weight,
    query_scale,
    query_keep,
    kv_weight,
    kv_scale,
    kv_keep,
    out_weight,
    out_scale,
    out_keep,
    documents,
):
    own_index = lax.axis_index("tp")
    local_rows = incoming[0]
    tok_count, own_width = local_rows.shape
    activ = local_rows.astype(jnp.float32)
    kv_width = KV_HEADS * HD
    group_size = HEADS // KV_HEADS
    partial_value = jnp.sum(activ * activ, axis=1, keepdims=True)
    squares = lax.psum(partial_value, "tp")
    normed = (activ * lax.rsqrt(squares / D + epsilon) * norm_gain[0].astype(jnp.float32)).astype(
        jnp.bfloat16
    )
    normed_all = lax.all_gather(normed, "tp", axis=1, tiled=True)
    q_eff = dequant(query_weight[0], query_scale[0], query_keep[0])
    q_columns = lax.all_to_all(q_eff, "tp", split_axis=1, concat_axis=0, tiled=True)
    q_width = q_columns.shape[1]
    queries = jnp.dot(normed_all, q_columns, preferred_element_type=jnp.float32)
    queries = rotate(queries, own_index * q_width).astype(jnp.bfloat16)
    kv_eff = dequant(kv_weight[0], kv_scale[0], kv_keep[0])
    kv_total = lax.psum(jnp.dot(normed, kv_eff, preferred_element_type=jnp.float32), "tp")
    keyval = rotate_keys(kv_total, 0, kv_width).astype(jnp.bfloat16)
    heads_here = q_width // HD
    kv_index = own_index * heads_here // group_size
    key_rows = lax.dynamic_slice_in_dim(keyval, kv_index * HD, HD, 1)
    value_rows = lax.dynamic_slice_in_dim(keyval, kv_width + kv_index * HD, HD, 1)
    token_ids = jnp.arange(tok_count, dtype=jnp.int32)
    allowed = (documents[:, None] == documents[None, :]) & (
        token_ids[:, None] >= token_ids[None, :]
    )
    query_three = queries.reshape(tok_count, heads_here, HD)
    scores = jnp.einsum(
        "thd,sd->hts", query_three, key_rows, preferred_element_type=jnp.float32
    ) / jnp.sqrt(jnp.float32(HD))
    exp_scores = jnp.where(allowed[None], jnp.exp(scores), jnp.float32(0.0))
    probs = (exp_scores / jnp.sum(exp_scores, axis=-1, keepdims=True)).astype(jnp.bfloat16)
    head_out = jnp.einsum("hts,sd->thd", probs, value_rows, preferred_element_type=jnp.float32)
    head_out = head_out.astype(jnp.bfloat16).reshape(tok_count, q_width)
    o_eff = dequant(out_weight[0], out_scale[0], out_keep[0])
    o_columns = lax.all_to_all(o_eff, "tp", split_axis=1, concat_axis=0, tiled=True)
    mixed_sum = jnp.dot(
        lax.all_gather(head_out, "tp", axis=1, tiled=True),
        o_columns,
        preferred_element_type=jnp.float32,
    )
    layer_out = (activ + mixed_sum).astype(jnp.bfloat16)
    received = passed_along(layer_out, "section", 1)
    return received[None]


def solution(mesh):
    placed = (
        P("section", None, "tp"),
        P("section", "tp"),
        P("section", "tp", None),
        P("section", "tp", None),
        P("section", "tp", None),
        P("section", "tp", None),
        P("section", "tp", None),
        P("section", "tp", None),
        P("section", "tp", None),
        P("section", "tp", None),
        P("section", "tp", None),
        P(),
    )
    return jax.shard_map(
        local, mesh=mesh, in_specs=placed, out_specs=P("section", None, "tp"), check_vma=False
    )
```

profile of v0, /device:TPU:1, one launch (start us, length us, event | category | flops | bytes accessed | tf_op | source)
XLA Modules:
  0.0 1547.2 jit_solution(16440638860779838320)
XLA Ops:
  7.6 163.6 %psum.14 = f32[320,1]{0,1:T(1,128)S(1)} all-reduce(f32[320,1]{0,1:T(1,128)S(1)} %broadcast_in_dim.16), channel_id=1, replica_groups=mesh['section'=8,'tp'=64] {'tp'}, use_global_device_ids=true, to_apply=%region_1.0 | all-reduce | flops 320 | bytes 2560 | tf_op jit(solution)/shard_map/psum | solution.py:73
  172.6 3.2 fusion.20
  177.4 3.2 copy.32
  182.5 5.6 all-to-all-start
  188.2 699.4 %all-reduce.2.cloned.1.call-done = f32[320,2048]{1,0:T(8,128)} async-done(((f32[320,2048]{1,0:T(8,128)}), f32[320,2048]{1,0:T(8,128)}) %all-reduce.2.cloned.1.call-update) | async-done | bytes 2621456 | tf_op jit(solution)/shard_map/psum | solution.py:84
  887.7 3.5 copy.27
  891.2 3.7 reshape.383
  894.9 4.1 fusion.55
  899.0 3.7 copy.39
  902.7 3.5 copy.40
  906.2 7.1 multiply_subtract_fusion
  918.0 2.7 copy.31
  920.7 2.8 select_convert_fusion
  923.5 3.2 copy.33
  926.7 2.9 copy.34
  929.6 3.2 dot_general.21
  932.8 255.4 %all-gather.4.cloned.1.call-done = bf16[320,8192]{1,0:T(8,128)(2,1)} async-done(((bf16[320,128]{1,0:T(8,128)(2,1)}), bf16[320,8192]{1,0:T(8,128)(2,1)}) %all-gather.4.cloned.1.call-update) | async-done | bytes 5242896 | tf_op jit(solution)/shard_map/all_gather | solution.py:77
  1188.2 5.1 fusion.2
  1197.0 3.4 copy.37
  1201.0 37.8 %all_to_all.32 = bf16[128,64,128]{0,2,1:T(8,128)(2,1)S(1)} all-to-all(bf16[128,64,128]{0,2,1:T(8,128)(2,1)S(1)} %fusion.4), channel_id=1, replica_groups=mesh['section'=8,'tp'=64] {'tp'}, dimensions={1} | all-to-all | bytes 4194304 | tf_op jit(solution)/shard_map/all_to_all | solution.py:103
  1238.8 2.9 copy.38
  1241.7 250.6 %all-gather.6.cloned.1.call-done = bf16[320,1,8192]{2,0,1:T(8,128)(2,1)} async-done(((bf16[320,1,128]{2,0,1:T(8,128)(2,1)}), bf16[320,1,8192]{2,0,1:T(8,128)(2,1)}) %all-gather.6.cloned.1.call-update) | async-done | bytes 5242896 | tf_op jit(solution)/shard_map/all_gather | solution.py:105
  1492.3 4.7 fusion.15
  1497.0 41.5 %collective-permute-start = (bf16[320,128]{1,0:T(8,128)(2,1)S(1)}, bf16[320,128]{1,0:T(8,128)(2,1)S(1)}, u32[]{:S(2)}, u32[]{:S(2)}) collective-permute-start(bf16[320,128]{1,0:T(8,128)(2,1)S(1)} %fusion.15), channel_id=1, source_target_pairs={{0,64},{64,128},{128,192},{192,256},{256,320},{320,384},{384,448},... | collective-permute-start | bytes 245768 | tf_op jit(solution)/shard_map/ppermute | solution.py:20
  (48 shorter events, 17.1 us)
Async XLA Ops:
  6.5 881.1 %all-reduce.2.cloned.1.call-start = ((), (), s32[]{:S(2)}) async-start(), calls=%async_computation.2 | async-start | bytes 5242880 | tf_op jit(solution)/shard_map/psum | solution.py:84
  175.7 0.9 copy-start.2
  175.8 1012.4 %all-gather.4.cloned.1.call-start = ((), (), s32[]{:S(2)}) async-start(), calls=%async_computation.3 | async-start | bytes 5324800 | tf_op jit(solution)/shard_map/all_gather | solution.py:77
  177.4 3.3 copy-start.4
  177.4 3.3 copy-start.5
  182.5 741.0 %all-to-all-start = ((bf16[128,64,128]{0,2,1:T(8,128)(2,1)}), bf16[128,64,128]{0,2,1:T(8,128)(2,1)}, u32[]{:S(2)}, u32[]{:S(2)}) async-start(bf16[128,64,128]{0,2,1:T(8,128)(2,1)} %fusion.5), calls=%async_computation | async-start | bytes 4194304 | tf_op jit(solution)/shard_map/all_to_all | solution.py:79
  188.1 1304.2 %all-gather.6.cloned.1.call-start = ((), (), s32[]{:S(2)}) async-start(), calls=%async_computation.4 | async-start | bytes 5324800 | tf_op jit(solution)/shard_map/all_gather | solution.py:105
  899.0 3.7 copy-start.1
  918.0 2.7 copy-start
  932.8 261.2 %copy-start.3 = (s32[320]{0:T(512)S(1)}, s32[320]{0:T(512)}, u32[]{:S(2)}) copy-start(s32[320]{0:T(512)} %param.23) | copy-start | bytes 3844
  1197.0 3.5 copy-start.6
  1197.0 3.5 copy-start.7
  1497.0 43.0 %collective-permute-start = (bf16[320,128]{1,0:T(8,128)(2,1)S(1)}, bf16[320,128]{1,0:T(8,128)(2,1)S(1)}, u32[]{:S(2)}, u32[]{:S(2)}) collective-permute-start(bf16[320,128]{1,0:T(8,128)(2,1)S(1)} %fusion.15), channel_id=1, source_target_pairs={{0,64},{64,128},{128,192},{192,256},{256,320},{320,384},{384,448},... | collective-permute-start | bytes 245768 | tf_op jit(solution)/shard_map/ppermute | solution.py:20
Sparse Core Ops, SparseCore 0:
  175.9 711.7 all-reduce.1
  889.7 298.4 all-gather.3
  1197.1 295.1 all-gather.5
where the time goes:
time: 1550 us
  waiting for transfers between devices  1210 us (78%)
  blocking collectives  201 us (13%)
  starting transfers between devices  47.2 us (3%)
  local copies, waits for them, and re-layouts  46.4 us (3%)
  other arithmetic  16 us (1%)
  matrix products  15.9 us (1%)
    psum x1, waiting for transfers between devices, local(): lax.psum(jnp.dot(normed, kv_eff, preferred_element_type=jnp.float32), 'tp')  699 us
    all_gather x1, waiting for transfers between devices, local(): normed_all = lax.all_gather(normed, 'tp', axis=1, tiled=True)  255 us
    all_gather x1, waiting for transfers between devices, local(): lax.all_gather(head_out, 'tp', axis=1, tiled=True)  251 us
    psum x1, blocking collectives, local(): squares = lax.psum(partial_value, 'tp')  164 us
    ppermute x1, starting transfers between devices, passed_along(): return lax.ppermute(value, axis, pairs)  41.5 us
    all_to_all x1, blocking collectives, local(): lax.all_to_all(o_eff, 'tp', split_axis=1, concat_axis=0, tiled=True)  37.8 us
  transfers between devices with their start and end apart: 5, of which 4 were waited for; matrix products, arithmetic and copies ran while one was open for 4% of the time, Pallas kernels for 0%

commit v1 on v0

--- a/solution.py
+++ b/solution.py
@@ -44,9 +44,26 @@
     return turned.reshape(row_count, col_count)
 
 
-def rotate_keys(values, first_col, kv_width):
-    col_ids = first_col + jnp.arange(values.shape[1], dtype=jnp.int32)
-    return jnp.where(col_ids[None, :] < kv_width, rotate(values, first_col), values)
+def gather_all(value, axis):
+    count = lax.axis_size(axis)
+    spread = jnp.broadcast_to(value[None], (count,) + value.shape)
+    return lax.all_to_all(spread, axis, 0, 0, tiled=True)
+
+
+def group_gather(value, axis, members):
+    count = lax.axis_size(axis)
+    own = lax.axis_index(axis)
+    held = value[None]
+    step = 1
+    while step < members:
+        pairs = [(source, source ^ step) for source in range(count)]
+        other = lax.ppermute(held, axis, pairs)
+        low = (own & step) == 0
+        held = jnp.where(
+            low, jnp.concatenate([held, other], 0), jnp.concatenate([other, held], 0)
+        )
+        step *= 2
+    return held
 
 
 def local(
@@ -63,30 +80,48 @@
     out_keep,
     documents,
 ):
+    tp = lax.axis_size("tp")
     own_index = lax.axis_index("tp")
     local_rows = incoming[0]
     tok_count, own_width = local_rows.shape
-    activ = local_rows.astype(jnp.float32)
     kv_width = KV_HEADS * HD
     group_size = HEADS // KV_HEADS
-    partial_value = jnp.sum(activ * activ, axis=1, keepdims=True)
-    squares = lax.psum(partial_value, "tp")
-    normed = (activ * lax.rsqrt(squares / D + epsilon) * norm_gain[0].astype(jnp.float32)).astype(
-        jnp.bfloat16
-    )
-    normed_all = lax.all_gather(normed, "tp", axis=1, tiled=True)
+    q_width = HEADS * HD // tp
+    heads_here = q_width // HD
+    members = group_size // heads_here
+    chunk = HD // members
+
     q_eff = dequant(query_weight[0], query_scale[0], query_keep[0])
     q_columns = lax.all_to_all(q_eff, "tp", split_axis=1, concat_axis=0, tiled=True)
-    q_width = q_columns.shape[1]
+    kv_eff = dequant(kv_weight[0], kv_scale[0], kv_keep[0])
+    kv_send = kv_eff.reshape(own_width, 2, KV_HEADS, members, chunk)
+    kv_send = kv_send.transpose(2, 3, 0, 1, 4).reshape(tp, own_width, 2 * chunk)
+    kv_columns = lax.all_to_all(kv_send, "tp", 0, 0, tiled=True)
+    o_eff = dequant(out_weight[0], out_scale[0], out_keep[0])
+    o_columns = lax.all_to_all(o_eff, "tp", split_axis=1, concat_axis=0, tiled=True)
+
+    extended = jnp.concatenate([local_rows, norm_gain[0][None]], axis=0)
+    gathered = gather_all(extended, "tp")
+    activ_all = gathered[:, :tok_count, :].astype(jnp.float32)
+    gain_all = gathered[:, tok_count, :].astype(jnp.float32)
+    squares = jnp.sum(activ_all * activ_all, axis=(0, 2))
+    scale_rows = lax.rsqrt(squares / D + epsilon)
+    normed_all = (activ_all * scale_rows[None, :, None] * gain_all[:, None, :]).astype(jnp.bfloat16)
+    normed_all = normed_all.transpose(1, 0, 2).reshape(tok_count, D)
+
     queries = jnp.dot(normed_all, q_columns, preferred_element_type=jnp.float32)
     queries = rotate(queries, own_index * q_width).astype(jnp.bfloat16)
-    kv_eff = dequant(kv_weight[0], kv_scale[0], kv_keep[0])
-    kv_total = lax.psum(jnp.dot(normed, kv_eff, preferred_element_type=jnp.float32), "tp")
-    keyval = rotate_keys(kv_total, 0, kv_width).astype(jnp.bfloat16)
-    heads_here = q_width // HD
-    kv_index = own_index * heads_here // group_size
-    key_rows = lax.dynamic_slice_in_dim(keyval, kv_index * HD, HD, 1)
-    value_rows = lax.dynamic_slice_in_dim(keyval, kv_width + kv_index * HD, HD, 1)
+
+    kv_part = jnp.dot(
+        normed_all, kv_columns.reshape(D, 2 * chunk), preferred_element_type=jnp.float32
+    )
+    member = own_index % members
+    key_part = rotate(kv_part[:, :chunk], member * chunk)
+    kv_part = jnp.concatenate([key_part, kv_part[:, chunk:]], axis=1).astype(jnp.bfloat16)
+    kv_group = group_gather(kv_part, "tp", members)
+    key_rows = kv_group[:, :, :chunk].transpose(1, 0, 2).reshape(tok_count, HD)
+    value_rows = kv_group[:, :, chunk:].transpose(1, 0, 2).reshape(tok_count, HD)
+
     token_ids = jnp.arange(tok_count, dtype=jnp.int32)
     allowed = (documents[:, None] == documents[None, :]) & (
         token_ids[:, None] >= token_ids[None, :]
@@ -99,14 +134,10 @@
     probs = (exp_scores / jnp.sum(exp_scores, axis=-1, keepdims=True)).astype(jnp.bfloat16)
     head_out = jnp.einsum("hts,sd->thd", probs, value_rows, preferred_element_type=jnp.float32)
     head_out = head_out.astype(jnp.bfloat16).reshape(tok_count, q_width)
-    o_eff = dequant(out_weight[0], out_scale[0], out_keep[0])
-    o_columns = lax.all_to_all(o_eff, "tp", split_axis=1, concat_axis=0, tiled=True)
-    mixed_sum = jnp.dot(
-        lax.all_gather(head_out, "tp", axis=1, tiled=True),
-        o_columns,
-        preferred_element_type=jnp.float32,
-    )
-    layer_out = (activ + mixed_sum).astype(jnp.bfloat16)
+
+    heads_all = gather_all(head_out, "tp").transpose(1, 0, 2).reshape(tok_count, tp * q_width)
+    mixed_sum = jnp.dot(heads_all, o_columns, preferred_element_type=jnp.float32)
+    layer_out = (local_rows.astype(jnp.float32) + mixed_sum).astype(jnp.bfloat16)
     received = passed_along(layer_out, "section", 1)
     return received[None]
 

time: 1550 us -> 429 us (0.28)
  waiting for transfers between devices: 1210 us -> 175 us
  blocking collectives: 201 us -> 126 us
    psum x1 -> x0, waiting for transfers between devices: 699 us -> none  [local(): lax.psum(jnp.dot(normed, kv_eff, preferred_element_type=jnp.float32), 'tp')]
    all_gather x2 -> x0, waiting for transfers between devices: 506 us -> none  [the longest x1 255 us: local(): normed_all = lax.all_gather(normed, 'tp', axis=1, tiled=True)]
    psum x1 -> x0, blocking collectives: 164 us -> none  [local(): squares = lax.psum(partial_value, 'tp')]
    all_to_all x0 -> x3, waiting for transfers between devices: none -> 119 us  [the longest x1 107 us: gather_all(): return lax.all_to_all(spread, axis, 0, 0, tiled=True)]
    all_to_all x1, blocking collectives: 37.8 us -> 126 us  [gather_all(): return lax.all_to_all(spread, axis, 0, 0, tiled=True)]
    all_to_all x1, waiting for transfers between devices: 0.01 us -> 49.6 us  [local(): lax.all_to_all(q_eff, 'tp', split_axis=1, concat_axis=0, tiled=True)]
    all_to_all x0 -> x3, starting transfers between devices: none -> 31.3 us  [the longest x1 12.5 us: local(): kv_columns = lax.all_to_all(kv_send, 'tp', 0, 0, tiled=True)]
    ppermute x1, starting transfers between devices: 41.5 us -> 11.8 us  [passed_along(): return lax.ppermute(value, axis, pairs)]
  transfers between devices with their start and end apart: 5 -> 8, of which waited for: 4 -> 6; matrix products, arithmetic and copies ran while one was open for 4% -> 13% of each run, Pallas kernels for 0% -> 0%
where the time goes in v1:
time: 429 us; the launch traced here: 428 us
  waiting for transfers between devices  175 us (41%)
  blocking collectives  126 us (29%)
  starting transfers between devices  58.5 us (14%)
  local copies, waits for them, and re-layouts  40.5 us (9%)
  other arithmetic  16.5 us (4%)
  matrix products  10.4 us (2%)
    all_to_all x1, blocking collectives, gather_all(): return lax.all_to_all(spread, axis, 0, 0, tiled=True)  126 us
    all_to_all x1, waiting for transfers between devices, gather_all(): return lax.all_to_all(spread, axis, 0, 0, tiled=True)  107 us
    all_to_all x1, waiting for transfers between devices, local(): lax.all_to_all(q_eff, 'tp', split_axis=1, concat_axis=0, tiled=True)  49.6 us
    all_to_all x1, starting transfers between devices, local(): kv_columns = lax.all_to_all(kv_send, 'tp', 0, 0, tiled=True)  12.5 us
    all_to_all x1, waiting for transfers between devices, local(): kv_columns = lax.all_to_all(kv_send, 'tp', 0, 0, tiled=True)  12.2 us
    all_to_all x1, starting transfers between devices, local(): lax.all_to_all(o_eff, 'tp', split_axis=1, concat_axis=0, tiled=True)  11.9 us
    ppermute x1, starting transfers between devices, passed_along(): return lax.ppermute(value, axis, pairs)  11.8 us
    ppermute x3, starting transfers between devices, group_gather(): other = lax.ppermute(held, axis, pairs)  10.1 us
  transfers between devices with their start and end apart: 8, of which 6 were waited for; matrix products, arithmetic and copies ran while one was open for 13% of the time, Pallas kernels for 0%

profile of v1, /device:TPU:1, one launch (start us, length us, event | category | flops | bytes accessed | tf_op | source)
XLA Modules:
  0.0 427.6 jit_solution(12733357945940257671)
XLA Ops:
  3.2 12.5 %all-to-all-start.1 = ((bf16[64,128,32]{1,2,0:T(8,128)(2,1)}), bf16[64,128,32]{1,2,0:T(8,128)(2,1)S(1)}, u32[]{:S(2)}, u32[]{:S(2)}) async-start(bf16[64,128,32]{1,2,0:T(8,128)(2,1)} %bitcast.5), calls=%async_computation.1 | async-start | bytes 1048576 | tf_op jit(solution)/shard_map/all_to_all | solution.py:99
  15.7 3.2 copy.50
  20.8 12.2 %all-to-all-done.1 = bf16[64,128,32]{1,2,0:T(8,128)(2,1)S(1)} async-done(((bf16[64,128,32]{1,2,0:T(8,128)(2,1)}), bf16[64,128,32]{1,2,0:T(8,128)(2,1)S(1)}, u32[]{:S(2)}, u32[]{:S(2)}) %all-to-all-start.1) | async-done | bytes 524320 | tf_op jit(solution)/shard_map/all_to_all | solution.py:99
  33.0 5.3 %all-to-all-start.2 = ((bf16[128,64,128]{0,2,1:T(8,128)(2,1)}), bf16[128,64,128]{0,2,1:T(8,128)(2,1)S(1)}, u32[]{:S(2)}, u32[]{:S(2)}) async-start(bf16[128,64,128]{0,2,1:T(8,128)(2,1)} %fusion.6), calls=%async_computation.2 | async-start | bytes 4194304 | tf_op jit(solution)/shard_map/all_to_all | solution.py:95
  38.3 49.6 %all-to-all-done.2 = bf16[128,64,128]{0,2,1:T(8,128)(2,1)S(1)} async-done(((bf16[128,64,128]{0,2,1:T(8,128)(2,1)}), bf16[128,64,128]{0,2,1:T(8,128)(2,1)S(1)}, u32[]{:S(2)}, u32[]{:S(2)}) %all-to-all-start.2) | async-done | bytes 2097184 | tf_op jit(solution)/shard_map/all_to_all | solution.py:95
  88.0 3.1 broadcast_in_dim.11
  91.1 6.9 %all-to-all-start = ((bf16[64,321,128]{2,1,0:T(8,128)(2,1)}), bf16[64,321,128]{2,1,0:T(8,128)(2,1)}, u32[]{:S(2)}, u32[]{:S(2)}) async-start(bf16[64,321,128]{2,1,0:T(8,128)(2,1)} %broadcast_in_dim.11), calls=%async_computation | async-start | bytes 10747904 | tf_op jit(solution)/shard_map/all_to_all | solution.py:50
  98.1 3.2 copy.55
  101.3 3.4 copy.56
  104.7 4.0 multiply_convert_fusion
  108.7 107.2 %all-to-all-done = bf16[64,321,128]{2,1,0:T(8,128)(2,1)} async-done(((bf16[64,321,128]{2,1,0:T(8,128)(2,1)}), bf16[64,321,128]{2,1,0:T(8,128)(2,1)}, u32[]{:S(2)}, u32[]{:S(2)}) %all-to-all-start) | async-done | bytes 5259296 | tf_op jit(solution)/shard_map/all_to_all | solution.py:50
  215.9 11.9 %all-to-all-start.4 = ((bf16[128,64,128]{2,0,1:T(8,128)(2,1)}), bf16[128,64,128]{2,0,1:T(8,128)(2,1)}, u32[]{:S(2)}, u32[]{:S(2)}) async-start(bf16[128,64,128]{2,0,1:T(8,128)(2,1)} %multiply_convert_fusion), calls=%async_computation.4 | async-start | bytes 4194304 | tf_op jit(solution)/shard_map/all_to_all | solution.py:101
  227.8 3.0 copy.51
  230.8 2.9 copy.52
  236.4 3.6 fusion
  241.0 4.4 %fusion.3 = bf16[320,64,128]{2,0,1:T(8,128)(2,1)S(1)} fusion(f32[64,128]{1,0:T(8,128)S(1)} %bitcast.90, f32[320]{0:T(512)S(1)} %add_rsqrt_fusion, bf16[64,321,128]{2,1,0:T(8,128)(2,1)} %all-to-all-done), kind=kLoop, calls=%fused_computation.5 | loop fusion | flops 10485760 | bytes 10519808 | tf_op jit(solution)/shard_map/transpose | solution.py:110
  245.4 5.7 %copy.49 = bf16[320,64,128]{2,1,0:T(8,128)(2,1)} copy(bf16[320,64,128]{2,0,1:T(8,128)(2,1)S(1)} %fusion.3) | data formatting | bytes 10485760 | tf_op jit(solution)/shard_map/transpose | solution.py:110
  255.8 8.8 %reshape.435 = bf16[320,8192,1]{1,0,2:T(8,128)(2,1)} reshape(bf16[320,64,128]{2,1,0:T(8,128)(2,1)} %copy.49) | data formatting | bytes 10485760 | tf_op jit(solution)/shard_map/reshape | solution.py:110
  264.6 5.1 %fusion.8 = f32[320,64,2]{0,1,2:T(8,128)S(1)} fusion(bf16[320,8192,1]{1,0,2:T(8,128)(2,1)} %reshape.435, bf16[64,2,8192]{2,1,0:T(2,128)(2,1)S(1)} %copy-done.2), kind=kOutput, calls=%fused_computation.12 | convolution fusion | flops 671088640 | bytes 7503872 | tf_op jit(solution)/shard_map/dot_general | solution.py:112
  269.8 4.3 %collective-permute-start.1 = (bf16[2,320,32]{1,2,0:T(8,128)(2,1)S(1)}, bf16[2,320,32]{1,2,0:T(8,128)(2,1)S(1)}, u32[]{:S(2)}, u32[]{:S(2)}) collective-permute-start(bf16[2,320,32]{1,2,0:T(8,128)(2,1)S(1)} %maximum_select_fusion.2), channel_id=1, source_target_pairs={{0,2},{1,3},{2,0},{3,1},{4,6},{5,7},{6,4},{7,5},{8,10},{9,11},{10,... | collective-permute-start | bytes 122888 | tf_op jit(solution)/shard_map/ppermute | solution.py:60
  276.9 3.0 collective-permute-start.2
  284.2 126.3 %all_to_all.44 = bf16[64,320,128]{2,1,0:T(8,128)(2,1)S(1)} all-to-all(bf16[64,320,128]{2,1,0:T(8,128)(2,1)S(1)} %broadcast_in_dim.14), channel_id=1, replica_groups=mesh['section'=8,'tp'=64] {'tp'}, dimensions={0} | all-to-all | bytes 10485760 | tf_op jit(solution)/shard_map/all_to_all | solution.py:50
  410.5 3.1 fusion.23
  413.7 11.8 %collective-permute-start.3 = (bf16[320,128]{1,0:T(8,128)(2,1)S(1)}, bf16[320,128]{1,0:T(8,128)(2,1)S(1)}, u32[]{:S(2)}, u32[]{:S(2)}) collective-permute-start(bf16[320,128]{1,0:T(8,128)(2,1)S(1)} %fusion.23), channel_id=1, source_target_pairs={{0,64},{64,128},{128,192},{192,256},{256,320},{320,384},{384,448},... | collective-permute-start | bytes 245768 | tf_op jit(solution)/shard_map/ppermute | solution.py:20
  (62 shorter events, 22.5 us)
Async XLA Ops:
  0.0 18.9 %copy-start.6 = (f32[1,1,64]{2,1,0:T(1,128)S(1)}, f32[1,1,64]{2,1,0:T(1,128)}, u32[]{:S(2)}) copy-start(f32[1,1,64]{2,1,0:T(1,128)} %param.15) | copy-start | bytes 772
  0.0 18.9 %copy-start.7 = (s32[1,1,64]{2,1,0:T(1,128)S(1)}, s32[1,1,64]{2,1,0:T(1,128)}, u32[]{:S(2)}) copy-start(s32[1,1,64]{2,1,0:T(1,128)} %param.16) | copy-start | bytes 772
  3.2 29.8 %all-to-all-start.1 = ((bf16[64,128,32]{1,2,0:T(8,128)(2,1)}), bf16[64,128,32]{1,2,0:T(8,128)(2,1)S(1)}, u32[]{:S(2)}, u32[]{:S(2)}) async-start(bf16[64,128,32]{1,2,0:T(8,128)(2,1)} %bitcast.5), calls=%async_computation.1 | async-start | bytes 1048576 | tf_op jit(solution)/shard_map/all_to_all | solution.py:99
  19.0 19.4 %copy-start.3 = (bf16[1,320,128]{2,1,0:T(8,128)(2,1)S(1)}, bf16[1,320,128]{2,1,0:T(8,128)(2,1)}, u32[]{:S(2)}) copy-start(bf16[1,320,128]{2,1,0:T(8,128)(2,1)} %param.12) | copy-start | bytes 245764
  19.0 19.4 %copy-start.4 = (bf16[1,128]{1,0:T(2,128)(2,1)S(1)}, bf16[1,128]{1,0:T(2,128)(2,1)}, u32[]{:S(2)}) copy-start(bf16[1,128]{1,0:T(2,128)(2,1)} %param.13) | copy-start | bytes 772
  33.0 55.0 %all-to-all-start.2 = ((bf16[128,64,128]{0,2,1:T(8,128)(2,1)}), bf16[128,64,128]{0,2,1:T(8,128)(2,1)S(1)}, u32[]{:S(2)}, u32[]{:S(2)}) async-start(bf16[128,64,128]{0,2,1:T(8,128)(2,1)} %fusion.6), calls=%async_computation.2 | async-start | bytes 4194304 | tf_op jit(solution)/shard_map/all_to_all | solution.py:95
  88.0 3.1 copy-start
  91.1 124.8 %all-to-all-start = ((bf16[64,321,128]{2,1,0:T(8,128)(2,1)}), bf16[64,321,128]{2,1,0:T(8,128)(2,1)}, u32[]{:S(2)}, u32[]{:S(2)}) async-start(bf16[64,321,128]{2,1,0:T(8,128)(2,1)} %broadcast_in_dim.11), calls=%async_computation | async-start | bytes 10747904 | tf_op jit(solution)/shard_map/all_to_all | solution.py:50
  98.1 6.6 %copy-start.8 = (f32[1,1,64]{2,1,0:T(1,128)S(1)}, f32[1,1,64]{2,1,0:T(1,128)}, u32[]{:S(2)}) copy-start(f32[1,1,64]{2,1,0:T(1,128)} %param.21) | copy-start | bytes 772
  98.1 6.6 %copy-start.9 = (s32[1,1,64]{2,1,0:T(1,128)S(1)}, s32[1,1,64]{2,1,0:T(1,128)}, u32[]{:S(2)}) copy-start(s32[1,1,64]{2,1,0:T(1,128)} %param.22) | copy-start | bytes 772
  104.7 123.2 %copy-start.1 = (bf16[128,64,128]{0,2,1:T(8,128)(2,1)S(1)}, bf16[128,64,128]{0,2,1:T(8,128)(2,1)}, u32[]{:S(2)}) copy-start(bf16[128,64,128]{0,2,1:T(8,128)(2,1)} %copy-done) | copy-start | bytes 6291460
  215.9 67.0 %all-to-all-start.4 = ((bf16[128,64,128]{2,0,1:T(8,128)(2,1)}), bf16[128,64,128]{2,0,1:T(8,128)(2,1)}, u32[]{:S(2)}, u32[]{:S(2)}) async-start(bf16[128,64,128]{2,0,1:T(8,128)(2,1)} %multiply_convert_fusion), calls=%async_computation.4 | async-start | bytes 4194304 | tf_op jit(solution)/shard_map/all_to_all | solution.py:101
  253.0 11.6 %copy-start.2 = (bf16[64,2,8192]{2,1,0:T(2,128)(2,1)S(1)}, bf16[64,2,8192]{2,1,0:T(2,128)(2,1)}, u32[]{:S(2)}) copy-start(bf16[64,2,8192]{2,1,0:T(2,128)(2,1)} %dot_general.21) | copy-start | bytes 6291460
  253.0 16.7 %collective-permute-start = (bf16[1,320,32]{1,2,0:T(8,128)(2,1)S(1)}, bf16[1,320,32]{1,2,0:T(8,128)(2,1)S(1)}, u32[]{:S(2)}, u32[]{:S(2)}) collective-permute-start(bf16[1,320,32]{1,2,0:T(8,128)(2,1)S(1)} %pad_maximum_fusion.2), channel_id=1, source_target_pairs={{0,1},{1,0},{2,3},{3,2},{4,5},{5,4},{6,7},{7,6},{8,9},{9,8},{10,11... | collective-permute-start | bytes 61448 | tf_op jit(solution)/shard_map/ppermute | solution.py:60
  264.6 17.7 %copy-start.5 = (s32[320]{0:T(512)S(1)}, s32[320]{0:T(512)}, u32[]{:S(2)}) copy-start(s32[320]{0:T(512)} %param.23) | copy-start | bytes 3844
  269.8 7.1 %collective-permute-start.1 = (bf16[2,320,32]{1,2,0:T(8,128)(2,1)S(1)}, bf16[2,320,32]{1,2,0:T(8,128)(2,1)S(1)}, u32[]{:S(2)}, u32[]{:S(2)}) collective-permute-start(bf16[2,320,32]{1,2,0:T(8,128)(2,1)S(1)} %maximum_select_fusion.2), channel_id=1, source_target_pairs={{0,2},{1,3},{2,0},{3,1},{4,6},{5,7},{6,4},{7,5},{8,10},{9,11},{10,... | collective-permute-start | bytes 122888 | tf_op jit(solution)/shard_map/ppermute | solution.py:60
  276.9 5.4 %collective-permute-start.2 = (bf16[4,320,32]{1,2,0:T(8,128)(2,1)S(1)}, bf16[4,320,32]{1,2,0:T(8,128)(2,1)S(1)}, u32[]{:S(2)}, u32[]{:S(2)}) collective-permute-start(bf16[4,320,32]{1,2,0:T(8,128)(2,1)S(1)} %maximum_select_fusion.1), channel_id=1, source_target_pairs={{0,4},{1,5},{2,6},{3,7},{4,0},{5,1},{6,2},{7,3},{8,12},{9,13},{10,... | collective-permute-start | bytes 245768 | tf_op jit(solution)/shard_map/ppermute | solution.py:60
  413.7 13.3 %collective-permute-start.3 = (bf16[320,128]{1,0:T(8,128)(2,1)S(1)}, bf16[320,128]{1,0:T(8,128)(2,1)S(1)}, u32[]{:S(2)}, u32[]{:S(2)}) collective-permute-start(bf16[320,128]{1,0:T(8,128)(2,1)S(1)} %fusion.23), channel_id=1, source_target_pairs={{0,64},{64,128},{128,192},{192,256},{256,320},{320,384},{384,448},... | collective-permute-start | bytes 245768 | tf_op jit(solution)/shard_map/ppermute | solution.py:20

commit v2 on v1

--- a/solution.py
+++ b/solution.py
@@ -1,6 +1,7 @@
 import jax
 import jax.numpy as jnp
 from jax import lax
+from jax.sharding import Mesh
 from jax.sharding import PartitionSpec as P
 
 D = 8192
@@ -44,10 +45,14 @@
     return turned.reshape(row_count, col_count)
 
 
-def gather_all(value, axis):
-    count = lax.axis_size(axis)
-    spread = jnp.broadcast_to(value[None], (count,) + value.shape)
-    return lax.all_to_all(spread, axis, 0, 0, tiled=True)
+def gather_all(value, axes):
+    held = value[None]
+    for axis in reversed(axes):
+        count = lax.axis_size(axis)
+        spread = jnp.broadcast_to(held[None], (count,) + held.shape)
+        held = lax.all_to_all(spread, axis, 0, 0, tiled=True)
+        held = held.reshape((-1,) + value.shape)
+    return held
 
 
 def group_gather(value, axis, members):
@@ -80,8 +85,8 @@
     out_keep,
     documents,
 ):
-    tp = lax.axis_size("tp")
-    own_index = lax.axis_index("tp")
+    tp = lax.axis_size(TP_AXES)
+    own_index = lax.axis_index(TP_AXES)
     local_rows = incoming[0]
     tok_count, own_width = local_rows.shape
     kv_width = KV_HEADS * HD
@@ -92,16 +97,16 @@
     chunk = HD // members
 
     q_eff = dequant(query_weight[0], query_scale[0], query_keep[0])
-    q_columns = lax.all_to_all(q_eff, "tp", split_axis=1, concat_axis=0, tiled=True)
+    q_columns = lax.all_to_all(q_eff, TP_AXES, split_axis=1, concat_axis=0, tiled=True)
     kv_eff = dequant(kv_weight[0], kv_scale[0], kv_keep[0])
     kv_send = kv_eff.reshape(own_width, 2, KV_HEADS, members, chunk)
     kv_send = kv_send.transpose(2, 3, 0, 1, 4).reshape(tp, own_width, 2 * chunk)
-    kv_columns = lax.all_to_all(kv_send, "tp", 0, 0, tiled=True)
+    kv_columns = lax.all_to_all(kv_send, TP_AXES, 0, 0, tiled=True)
     o_eff = dequant(out_weight[0], out_scale[0], out_keep[0])
-    o_columns = lax.all_to_all(o_eff, "tp", split_axis=1, concat_axis=0, tiled=True)
+    o_columns = lax.all_to_all(o_eff, TP_AXES, split_axis=1, concat_axis=0, tiled=True)
 
     extended = jnp.concatenate([local_rows, norm_gain[0][None]], axis=0)
-    gathered = gather_all(extended, "tp")
+    gathered = gather_all(extended, TP_AXES)
     activ_all = gathered[:, :tok_count, :].astype(jnp.float32)
     gain_all = gathered[:, tok_count, :].astype(jnp.float32)
     squares = jnp.sum(activ_all * activ_all, axis=(0, 2))
@@ -118,7 +123,7 @@
     member = own_index % members
     key_part = rotate(kv_part[:, :chunk], member * chunk)
     kv_part = jnp.concatenate([key_part, kv_part[:, chunk:]], axis=1).astype(jnp.bfloat16)
-    kv_group = group_gather(kv_part, "tp", members)
+    kv_group = group_gather(kv_part, TP_AXES, members)
     key_rows = kv_group[:, :, :chunk].transpose(1, 0, 2).reshape(tok_count, HD)
     value_rows = kv_group[:, :, chunk:].transpose(1, 0, 2).reshape(tok_count, HD)
 
@@ -135,28 +140,34 @@
     head_out = jnp.einsum("hts,sd->thd", probs, value_rows, preferred_element_type=jnp.float32)
     head_out = head_out.astype(jnp.bfloat16).reshape(tok_count, q_width)
 
-    heads_all = gather_all(head_out, "tp").transpose(1, 0, 2).reshape(tok_count, tp * q_width)
+    heads_all = gather_all(head_out, TP_AXES).transpose(1, 0, 2).reshape(tok_count, tp * q_width)
     mixed_sum = jnp.dot(heads_all, o_columns, preferred_element_type=jnp.float32)
     layer_out = (local_rows.astype(jnp.float32) + mixed_sum).astype(jnp.bfloat16)
     received = passed_along(layer_out, "section", 1)
     return received[None]
 
 
+TP_AXES = ("tp_x", "tp_z", "tp_y")
+
+
 def solution(mesh):
+    devices = mesh.devices.reshape(mesh.shape["section"], 4, 4, -1)
+    mesh = Mesh(devices, ("section",) + TP_AXES)
+    tp = TP_AXES
     placed = (
-        P("section", None, "tp"),
-        P("section", "tp"),
-        P("section", "tp", None),
-        P("section", "tp", None),
-        P("section", "tp", None),
-        P("section", "tp", None),
-        P("section", "tp", None),
-        P("section", "tp", None),
-        P("section", "tp", None),
-        P("section", "tp", None),
-        P("section", "tp", None),
+        P("section", None, tp),
+        P("section", tp),
+        P("section", tp, None),
+        P("section", tp, None),
+        P("section", tp, None),
+        P("section", tp, None),
+        P("section", tp, None),
+        P("section", tp, None),
+        P("section", tp, None),
+        P("section", tp, None),
+        P("section", tp, None),
         P(),
     )
     return jax.shard_map(
-        local, mesh=mesh, in_specs=placed, out_specs=P("section", None, "tp"), check_vma=False
+        local, mesh=mesh, in_specs=placed, out_specs=P("section", None, tp), check_vma=False
     )

time: 429 us -> 374 us (0.87)
  waiting for transfers between devices: 175 us -> 141 us
  blocking collectives: 126 us -> 115 us
  starting transfers between devices: 58.5 us -> 52.4 us
  other arithmetic: 16.5 us -> 11.2 us
    all_to_all x4 -> x5, waiting for transfers between devices: 169 us -> 137 us  [the longest x2 82 us: gather_all(): held = lax.all_to_all(spread, axis, 0, 0, tiled=True)]
    all_to_all x1 -> x4, blocking collectives: 126 us -> 115 us  [gather_all(): held = lax.all_to_all(spread, axis, 0, 0, tiled=True)]
    all_to_all x4 -> x5, starting transfers between devices: 36.7 us -> 30.8 us  [the longest x2 11.4 us: gather_all(): held = lax.all_to_all(spread, axis, 0, 0, tiled=True)]
    transpose x1 -> x0, local copies, waits for them, and re-layouts: 5.74 us -> none  [local(): normed_all = normed_all.transpose(1, 0, 2).reshape(tok_count, D)]
    all_to_all x1 -> x3, local copies, waits for them, and re-layouts: 2.99 us -> 7.56 us  [the longest x2 4.34 us: gather_all(): held = lax.all_to_all(spread, axis, 0, 0, tiled=True)]
  transfers between devices with their start and end apart: 8 -> 9, of which waited for: 6 -> 7; matrix products, arithmetic and copies ran while one was open for 13% -> 14% of each run, Pallas kernels for 0% -> 0%
where the time goes in v2:
time: 374 us; the launch traced here: 373 us
  waiting for transfers between devices  141 us (38%)
  blocking collectives  115 us (31%)
  starting transfers between devices  52.4 us (14%)
  local copies, waits for them, and re-layouts  41 us (11%)
  matrix products  11.9 us (3%)
  other arithmetic  11.2 us (3%)
    all_to_all x4, blocking collectives, gather_all(): held = lax.all_to_all(spread, axis, 0, 0, tiled=True)  115 us
    all_to_all x2, waiting for transfers between devices, gather_all(): held = lax.all_to_all(spread, axis, 0, 0, tiled=True)  82 us
    all_to_all x1, waiting for transfers between devices, local(): lax.all_to_all(q_eff, TP_AXES, split_axis=1, concat_axis=0, tiled=True)  38.2 us
    all_to_all x1, waiting for transfers between devices, local(): kv_columns = lax.all_to_all(kv_send, TP_AXES, 0, 0, tiled=True)  16 us
    ppermute x1, starting transfers between devices, passed_along(): return lax.ppermute(value, axis, pairs)  11.9 us
    all_to_all x2, starting transfers between devices, gather_all(): held = lax.all_to_all(spread, axis, 0, 0, tiled=True)  11.4 us
    ppermute x3, starting transfers between devices, group_gather(): other = lax.ppermute(held, axis, pairs)  9.71 us
    reshape x1, local copies, waits for them, and re-layouts, local(): normed_all = normed_all.transpose(1, 0, 2).reshape(tok_count, D)  8.8 us
  transfers between devices with their start and end apart: 9, of which 7 were waited for; matrix products, arithmetic and copies ran while one was open for 14% of the time, Pallas kernels for 0%

profile of v2, /device:TPU:1, one launch (start us, length us, event | category | flops | bytes accessed | tf_op | source)
XLA Modules:
  0.0 372.7 jit_solution(15502187405280550151)
XLA Ops:
  1.0 10.7 %all_to_all.64 = bf16[4,1,321,128]{3,2,1,0:T(8,128)(2,1)S(1)} all-to-all(bf16[4,1,321,128]{3,2,1,0:T(8,128)(2,1)S(1)} %broadcast_in_dim.28), channel_id=1, replica_groups=mesh['section'=8,'tp_x'=4,'tp_z'=4,'tp_y'=4] {'tp_y'}, dimensions={0} | all-to-all | bytes 657408 | tf_op jit(solution)/shard_map/all_to_all | solution.py:53
  13.3 6.3 %all-to-all-start.1 = ((bf16[4,4,321,128]{3,1,2,0:T(4,128)(2,1)}), bf16[4,4,321,128]{3,1,2,0:T(4,128)(2,1)S(1)}, u32[]{:S(2)}, u32[]{:S(2)}) async-start(bf16[4,4,321,128]{3,1,2,0:T(4,128)(2,1)} %broadcast_in_dim.30), calls=%async_computation.1 | async-start | bytes 2629632 | tf_op jit(solution)/shard_map/all_to_all | solution.py:53
  21.0 29.6 %all-to-all-done.1 = bf16[4,4,321,128]{3,1,2,0:T(4,128)(2,1)S(1)} async-done(((bf16[4,4,321,128]{3,1,2,0:T(4,128)(2,1)}), bf16[4,4,321,128]{3,1,2,0:T(4,128)(2,1)S(1)}, u32[]{:S(2)}, u32[]{:S(2)}) %all-to-all-start.1) | async-done | bytes 1314848 | tf_op jit(solution)/shard_map/all_to_all | solution.py:53
  50.6 5.6 %all-to-all-start.3 = ((bf16[64,128,32]{1,2,0:T(8,128)(2,1)}), bf16[64,128,32]{1,2,0:T(8,128)(2,1)S(1)}, u32[]{:S(2)}, u32[]{:S(2)}) async-start(bf16[64,128,32]{1,2,0:T(8,128)(2,1)} %bitcast.8), calls=%async_computation.3 | async-start | bytes 1048576 | tf_op jit(solution)/shard_map/all_to_all | solution.py:104
  56.6 16.0 %all-to-all-done.3 = bf16[64,128,32]{1,2,0:T(8,128)(2,1)S(1)} async-done(((bf16[64,128,32]{1,2,0:T(8,128)(2,1)}), bf16[64,128,32]{1,2,0:T(8,128)(2,1)S(1)}, u32[]{:S(2)}, u32[]{:S(2)}) %all-to-all-start.3) | async-done | bytes 524320 | tf_op jit(solution)/shard_map/all_to_all | solution.py:104
  75.6 5.1 %all-to-all-start.2 = ((bf16[4,16,321,128]{3,1,2,0:T(8,128)(2,1)}), bf16[4,16,321,128]{3,1,2,0:T(8,128)(2,1)}, u32[]{:S(2)}, u32[]{:S(2)}) async-start(bf16[4,16,321,128]{3,1,2,0:T(8,128)(2,1)} %broadcast_in_dim.32), calls=%async_computation.2 | async-start | bytes 10518528 | tf_op jit(solution)/shard_map/all_to_all | solution.py:53
  80.7 3.2 copy.83
  85.8 52.4 %all-to-all-done.2 = bf16[4,16,321,128]{3,1,2,0:T(8,128)(2,1)} async-done(((bf16[4,16,321,128]{3,1,2,0:T(8,128)(2,1)}), bf16[4,16,321,128]{3,1,2,0:T(8,128)(2,1)}, u32[]{:S(2)}, u32[]{:S(2)}) %all-to-all-start.2) | async-done | bytes 5259296 | tf_op jit(solution)/shard_map/all_to_all | solution.py:53
  138.2 6.5 %all-to-all-start.4 = ((bf16[128,64,128]{0,2,1:T(8,128)(2,1)}), bf16[128,64,128]{0,2,1:T(8,128)(2,1)}, u32[]{:S(2)}, u32[]{:S(2)}) async-start(bf16[128,64,128]{0,2,1:T(8,128)(2,1)} %fusion.6), calls=%async_computation.4 | async-start | bytes 4194304 | tf_op jit(solution)/shard_map/all_to_all | solution.py:100
  144.7 3.2 copy.88
  147.9 3.5 copy.89
  151.4 3.9 %multiply_convert_fusion = bf16[128,64,128]{2,0,1:T(8,128)(2,1)} fusion(f32[128,64,128]{2,0,1:T(8,128)} %copy.89, f32[64]{0:T(128)S(1)} %multiply_bitcast_fusion), kind=kLoop, calls=%fused_computation.10 | loop fusion | flops 2097152 | bytes 6291712 | tf_op jit(solution)/shard_map/convert_element_type | solution.py:29
  155.3 38.2 %all-to-all-done.4 = bf16[128,64,128]{0,2,1:T(8,128)(2,1)} async-done(((bf16[128,64,128]{0,2,1:T(8,128)(2,1)}), bf16[128,64,128]{0,2,1:T(8,128)(2,1)}, u32[]{:S(2)}, u32[]{:S(2)}) %all-to-all-start.4) | async-done | bytes 2097184 | tf_op jit(solution)/shard_map/all_to_all | solution.py:100
  193.5 7.3 %all-to-all-start.8 = ((bf16[128,64,128]{2,0,1:T(8,128)(2,1)}), bf16[128,64,128]{2,0,1:T(8,128)(2,1)}, u32[]{:S(2)}, u32[]{:S(2)}) async-start(bf16[128,64,128]{2,0,1:T(8,128)(2,1)} %multiply_convert_fusion), calls=%async_computation.8 | async-start | bytes 4194304 | tf_op jit(solution)/shard_map/all_to_all | solution.py:106
  200.9 4.2 %copy.76 = bf16[4,16,321,128]{3,1,0,2:T(8,128)(2,1)S(1)} copy(bf16[4,16,321,128]{3,1,2,0:T(8,128)(2,1)} %all-to-all-done.2) | data formatting | bytes 10518528 | tf_op jit(solution)/shard_map/all_to_all | solution.py:53
  217.7 5.1 %collective-permute-start.1 = (bf16[2,320,32]{1,2,0:T(8,128)(2,1)S(1)}, bf16[2,320,32]{1,2,0:T(8,128)(2,1)S(1)}, u32[]{:S(2)}, u32[]{:S(2)}) collective-permute-start(bf16[2,320,32]{1,2,0:T(8,128)(2,1)S(1)} %maximum_select_fusion.2), channel_id=1, source_target_pairs={{0,2},{1,3},{2,0},{3,1},{4,6},{5,7},{6,4},{7,5},{8,10},{9,11},{10,... | collective-permute-start | bytes 122888 | tf_op jit(solution)/shard_map/ppermute | solution.py:65
  222.9 8.8 %reshape.451 = bf16[320,8192,1]{1,0,2:T(8,128)(2,1)} reshape(bf16[320,64,128]{2,1,0:T(8,128)(2,1)} %copy-done) | data formatting | bytes 10485760 | tf_op jit(solution)/shard_map/reshape | solution.py:115
  233.7 3.2 copy.84
  239.9 3.2 dot_general.21
  243.0 5.1 %fusion.9 = f32[320,64,2]{0,1,2:T(8,128)S(1)} fusion(bf16[320,8192,1]{1,0,2:T(8,128)(2,1)} %reshape.451, bf16[64,2,8192]{2,1,0:T(2,128)(2,1)S(1)} %dot_general.21), kind=kOutput, calls=%fused_computation.13 | convolution fusion | flops 671088640 | bytes 7503872 | tf_op jit(solution)/shard_map/dot_general | solution.py:117
  250.0 8.3 %all_to_all.65 = bf16[4,1,320,128]{3,2,1,0:T(8,128)(2,1)S(1)} all-to-all(bf16[4,1,320,128]{3,2,1,0:T(8,128)(2,1)S(1)} %broadcast_in_dim.35), channel_id=1, replica_groups=mesh['section'=8,'tp_x'=4,'tp_z'=4,'tp_y'=4] {'tp_y'}, dimensions={0} | all-to-all | bytes 655360 | tf_op jit(solution)/shard_map/all_to_all | solution.py:53
  258.5 35.2 %all_to_all.66 = bf16[4,4,320,128]{3,2,1,0:T(8,128)(2,1)S(1)} all-to-all(bf16[4,4,320,128]{3,2,1,0:T(8,128)(2,1)S(1)} %broadcast_in_dim.72), channel_id=1, replica_groups=mesh['section'=8,'tp_x'=4,'tp_z'=4,'tp_y'=4] {'tp_z'}, dimensions={0} | all-to-all | bytes 2621440 | tf_op jit(solution)/shard_map/all_to_all | solution.py:53
  295.0 60.5 %all_to_all.67 = bf16[4,16,320,128]{3,2,1,0:T(8,128)(2,1)S(1)} all-to-all(bf16[4,16,320,128]{3,2,1,0:T(8,128)(2,1)S(1)} %broadcast_in_dim.74), channel_id=1, replica_groups=mesh['section'=8,'tp_x'=4,'tp_z'=4,'tp_y'=4] {'tp_x'}, dimensions={0} | all-to-all | bytes 10485760 | tf_op jit(solution)/shard_map/all_to_all | solution.py:53
  358.7 11.9 %collective-permute-start.3 = (bf16[320,128]{1,0:T(8,128)(2,1)S(1)}, bf16[320,128]{1,0:T(8,128)(2,1)S(1)}, u32[]{:S(2)}, u32[]{:S(2)}) collective-permute-start(bf16[320,128]{1,0:T(8,128)(2,1)S(1)} %fusion.20), channel_id=1, source_target_pairs={{0,64},{64,128},{128,192},{192,256},{256,320},{320,384},{384,448},... | collective-permute-start | bytes 245768 | tf_op jit(solution)/shard_map/ppermute | solution.py:21
  (74 shorter events, 35.2 us)
Async XLA Ops:
  0.0 19.6 %copy-start.1 = (bf16[1,128,2048]{2,1,0:T(8,128)(2,1)S(1)}, bf16[1,128,2048]{2,1,0:T(8,128)(2,1)}, u32[]{:S(2)}) copy-start(bf16[1,128,2048]{2,1,0:T(8,128)(2,1)} %param.17) | copy-start | bytes 1572868
  0.0 19.9 %copy-start.4 = (f32[1,1,16]{2,1,0:T(1,128)S(1)}, f32[1,1,16]{2,1,0:T(1,128)}, u32[]{:S(2)}) copy-start(f32[1,1,16]{2,1,0:T(1,128)} %param.18) | copy-start | bytes 196
  0.0 19.9 %copy-start.5 = (s32[1,1,16]{2,1,0:T(1,128)S(1)}, s32[1,1,16]{2,1,0:T(1,128)}, u32[]{:S(2)}) copy-start(s32[1,1,16]{2,1,0:T(1,128)} %param.19) | copy-start | bytes 196
  13.3 37.3 %all-to-all-start.1 = ((bf16[4,4,321,128]{3,1,2,0:T(4,128)(2,1)}), bf16[4,4,321,128]{3,1,2,0:T(4,128)(2,1)S(1)}, u32[]{:S(2)}, u32[]{:S(2)}) async-start(bf16[4,4,321,128]{3,1,2,0:T(4,128)(2,1)} %broadcast_in_dim.30), calls=%async_computation.1 | async-start | bytes 2629632 | tf_op jit(solution)/shard_map/all_to_all | solution.py:53
  50.6 22.0 %all-to-all-start.3 = ((bf16[64,128,32]{1,2,0:T(8,128)(2,1)}), bf16[64,128,32]{1,2,0:T(8,128)(2,1)S(1)}, u32[]{:S(2)}, u32[]{:S(2)}) async-start(bf16[64,128,32]{1,2,0:T(8,128)(2,1)} %bitcast.8), calls=%async_computation.3 | async-start | bytes 1048576 | tf_op jit(solution)/shard_map/all_to_all | solution.py:104
  75.6 62.5 %all-to-all-start.2 = ((bf16[4,16,321,128]{3,1,2,0:T(8,128)(2,1)}), bf16[4,16,321,128]{3,1,2,0:T(8,128)(2,1)}, u32[]{:S(2)}, u32[]{:S(2)}) async-start(bf16[4,16,321,128]{3,1,2,0:T(8,128)(2,1)} %broadcast_in_dim.32), calls=%async_computation.2 | async-start | bytes 10518528 | tf_op jit(solution)/shard_map/all_to_all | solution.py:53
  80.7 3.3 copy-start.6
  80.7 3.3 copy-start.7
  138.2 55.4 %all-to-all-start.4 = ((bf16[128,64,128]{0,2,1:T(8,128)(2,1)}), bf16[128,64,128]{0,2,1:T(8,128)(2,1)}, u32[]{:S(2)}, u32[]{:S(2)}) async-start(bf16[128,64,128]{0,2,1:T(8,128)(2,1)} %fusion.6), calls=%async_computation.4 | async-start | bytes 4194304 | tf_op jit(solution)/shard_map/all_to_all | solution.py:100
  147.9 3.5 copy-start.8
  147.9 3.5 copy-start.9
  193.5 56.4 %all-to-all-start.8 = ((bf16[128,64,128]{2,0,1:T(8,128)(2,1)}), bf16[128,64,128]{2,0,1:T(8,128)(2,1)}, u32[]{:S(2)}, u32[]{:S(2)}) async-start(bf16[128,64,128]{2,0,1:T(8,128)(2,1)} %multiply_convert_fusion), calls=%async_computation.8 | async-start | bytes 4194304 | tf_op jit(solution)/shard_map/all_to_all | solution.py:106
  208.6 3.1 copy-start
  212.0 5.7 %collective-permute-start = (bf16[1,320,32]{1,2,0:T(8,128)(2,1)S(1)}, bf16[1,320,32]{1,2,0:T(8,128)(2,1)S(1)}, u32[]{:S(2)}, u32[]{:S(2)}) collective-permute-start(bf16[1,320,32]{1,2,0:T(8,128)(2,1)S(1)} %pad_maximum_fusion.2), channel_id=1, source_target_pairs={{0,1},{1,0},{2,3},{3,2},{4,5},{5,4},{6,7},{7,6},{8,9},{9,8},{10,11... | collective-permute-start | bytes 61448 | tf_op jit(solution)/shard_map/ppermute | solution.py:65
  217.7 14.0 %collective-permute-start.1 = (bf16[2,320,32]{1,2,0:T(8,128)(2,1)S(1)}, bf16[2,320,32]{1,2,0:T(8,128)(2,1)S(1)}, u32[]{:S(2)}, u32[]{:S(2)}) collective-permute-start(bf16[2,320,32]{1,2,0:T(8,128)(2,1)S(1)} %maximum_select_fusion.2), channel_id=1, source_target_pairs={{0,2},{1,3},{2,0},{3,1},{4,6},{5,7},{6,4},{7,5},{8,10},{9,11},{10,... | collective-permute-start | bytes 122888 | tf_op jit(solution)/shard_map/ppermute | solution.py:65
  231.7 17.1 %collective-permute-start.2 = (bf16[4,320,32]{1,2,0:T(8,128)(2,1)S(1)}, bf16[4,320,32]{1,2,0:T(8,128)(2,1)S(1)}, u32[]{:S(2)}, u32[]{:S(2)}) collective-permute-start(bf16[4,320,32]{1,2,0:T(8,128)(2,1)S(1)} %maximum_select_fusion.1), channel_id=1, source_target_pairs={{0,4},{1,5},{2,6},{3,7},{4,0},{5,1},{6,2},{7,3},{8,12},{9,13},{10,... | collective-permute-start | bytes 245768 | tf_op jit(solution)/shard_map/ppermute | solution.py:65
  243.0 5.9 %copy-start.3 = (s32[320]{0:T(512)S(1)}, s32[320]{0:T(512)}, u32[]{:S(2)}) copy-start(s32[320]{0:T(512)} %param.23) | copy-start | bytes 3844
  295.0 60.5 %copy-start.2 = (bf16[1,320,128]{2,1,0:T(8,128)(2,1)S(1)}, bf16[1,320,128]{2,1,0:T(8,128)(2,1)}, u32[]{:S(2)}) copy-start(bf16[1,320,128]{2,1,0:T(8,128)(2,1)} %param.12) | copy-start | bytes 245764
  358.7 13.4 %collective-permute-start.3 = (bf16[320,128]{1,0:T(8,128)(2,1)S(1)}, bf16[320,128]{1,0:T(8,128)(2,1)S(1)}, u32[]{:S(2)}, u32[]{:S(2)}) collective-permute-start(bf16[320,128]{1,0:T(8,128)(2,1)S(1)} %fusion.20), channel_id=1, source_target_pairs={{0,64},{64,128},{128,192},{192,256},{256,320},{320,384},{384,448},... | collective-permute-start | bytes 245768 | tf_op jit(solution)/shard_map/ppermute | solution.py:21

commit v3 on v2

--- a/solution.py
+++ b/solution.py
@@ -87,42 +87,53 @@
 ):
     tp = lax.axis_size(TP_AXES)
     own_index = lax.axis_index(TP_AXES)
+    planes = lax.axis_size(CROSS)
+    plane = lax.axis_size(PLANE)
     local_rows = incoming[0]
     tok_count, own_width = local_rows.shape
-    kv_width = KV_HEADS * HD
     group_size = HEADS // KV_HEADS
     q_width = HEADS * HD // tp
     heads_here = q_width // HD
     members = group_size // heads_here
     chunk = HD // members
+    halves = plane // members
 
     q_eff = dequant(query_weight[0], query_scale[0], query_keep[0])
-    q_columns = lax.all_to_all(q_eff, TP_AXES, split_axis=1, concat_axis=0, tiled=True)
+    q_send = q_eff.reshape(own_width, planes, plane, q_width).transpose(2, 0, 1, 3)
+    q_rows = lax.all_to_all(q_send, PLANE, 0, 0, tiled=True)
+    q_rows = q_rows.reshape(plane * own_width, planes * q_width)
     kv_eff = dequant(kv_weight[0], kv_scale[0], kv_keep[0])
-    kv_send = kv_eff.reshape(own_width, 2, KV_HEADS, members, chunk)
-    kv_send = kv_send.transpose(2, 3, 0, 1, 4).reshape(tp, own_width, 2 * chunk)
-    kv_columns = lax.all_to_all(kv_send, TP_AXES, 0, 0, tiled=True)
+    kv_send = kv_eff.reshape(own_width, 2, planes, halves, members, chunk)
+    kv_send = kv_send.transpose(3, 4, 0, 2, 1, 5).reshape(plane, own_width, planes * 2 * chunk)
+    kv_rows = lax.all_to_all(kv_send, PLANE, 0, 0, tiled=True)
+    kv_rows = kv_rows.reshape(plane * own_width, planes * 2 * chunk)
     o_eff = dequant(out_weight[0], out_scale[0], out_keep[0])
-    o_columns = lax.all_to_all(o_eff, TP_AXES, split_axis=1, concat_axis=0, tiled=True)
+    o_send = o_eff.reshape(q_width, planes, plane, own_width).transpose(2, 0, 1, 3)
+    o_rows = lax.all_to_all(o_send, PLANE, 0, 0, tiled=True)
+    o_rows = o_rows.reshape(plane * q_width, planes * own_width)
 
     extended = jnp.concatenate([local_rows, norm_gain[0][None]], axis=0)
-    gathered = gather_all(extended, TP_AXES)
-    activ_all = gathered[:, :tok_count, :].astype(jnp.float32)
-    gain_all = gathered[:, tok_count, :].astype(jnp.float32)
-    squares = jnp.sum(activ_all * activ_all, axis=(0, 2))
+    gathered = gather_all(extended, PLANE)
+    activ_pl = gathered[:, :tok_count, :].astype(jnp.float32)
+    gain_pl = gathered[:, tok_count, :].astype(jnp.float32)
+    partial_sq = jnp.sum(activ_pl * activ_pl, axis=(0, 2))
+    squares = jnp.sum(gather_all(partial_sq, (CROSS,)), axis=0)
     scale_rows = lax.rsqrt(squares / D + epsilon)
-    normed_all = (activ_all * scale_rows[None, :, None] * gain_all[:, None, :]).astype(jnp.bfloat16)
-    normed_all = normed_all.transpose(1, 0, 2).reshape(tok_count, D)
+    normed_pl = (activ_pl * scale_rows[None, :, None] * gain_pl[:, None, :]).astype(jnp.bfloat16)
+    normed_pl = normed_pl.transpose(1, 0, 2).reshape(tok_count, plane * own_width)
 
-    queries = jnp.dot(normed_all, q_columns, preferred_element_type=jnp.float32)
-    queries = rotate(queries, own_index * q_width).astype(jnp.bfloat16)
+    q_part = jnp.dot(normed_pl, q_rows, preferred_element_type=jnp.float32)
+    kv_part = jnp.dot(normed_pl, kv_rows, preferred_element_type=jnp.float32)
+    packed = jnp.concatenate(
+        [q_part.reshape(tok_count, planes, q_width), kv_part.reshape(tok_count, planes, 2 * chunk)],
+        axis=2,
+    ).transpose(1, 0, 2)
+    summed = jnp.sum(lax.all_to_all(packed, CROSS, 0, 0, tiled=True), axis=0)
 
-    kv_part = jnp.dot(
-        normed_all, kv_columns.reshape(D, 2 * chunk), preferred_element_type=jnp.float32
-    )
+    queries = rotate(summed[:, :q_width], own_index * q_width).astype(jnp.bfloat16)
     member = own_index % members
-    key_part = rotate(kv_part[:, :chunk], member * chunk)
-    kv_part = jnp.concatenate([key_part, kv_part[:, chunk:]], axis=1).astype(jnp.bfloat16)
+    key_part = rotate(summed[:, q_width : q_width + chunk], member * chunk)
+    kv_part = jnp.concatenate([key_part, summed[:, q_width + chunk :]], axis=1).astype(jnp.bfloat16)
     kv_group = group_gather(kv_part, TP_AXES, members)
     key_rows = kv_group[:, :, :chunk].transpose(1, 0, 2).reshape(tok_count, HD)
     value_rows = kv_group[:, :, chunk:].transpose(1, 0, 2).reshape(tok_count, HD)
@@ -140,14 +151,18 @@
     head_out = jnp.einsum("hts,sd->thd", probs, value_rows, preferred_element_type=jnp.float32)
     head_out = head_out.astype(jnp.bfloat16).reshape(tok_count, q_width)
 
-    heads_all = gather_all(head_out, TP_AXES).transpose(1, 0, 2).reshape(tok_count, tp * q_width)
-    mixed_sum = jnp.dot(heads_all, o_columns, preferred_element_type=jnp.float32)
+    heads_pl = gather_all(head_out, PLANE).transpose(1, 0, 2).reshape(tok_count, plane * q_width)
+    out_part = jnp.dot(heads_pl, o_rows, preferred_element_type=jnp.float32)
+    out_part = out_part.reshape(tok_count, planes, own_width).transpose(1, 0, 2)
+    mixed_sum = jnp.sum(lax.all_to_all(out_part, CROSS, 0, 0, tiled=True), axis=0)
     layer_out = (local_rows.astype(jnp.float32) + mixed_sum).astype(jnp.bfloat16)
     received = passed_along(layer_out, "section", 1)
     return received[None]
 
 
 TP_AXES = ("tp_x", "tp_z", "tp_y")
+CROSS = "tp_x"
+PLANE = ("tp_z", "tp_y")
 
 
 def solution(mesh):

time: 374 us -> 305 us (0.82)
  blocking collectives: 115 us -> 22.6 us
  starting transfers between devices: 52.4 us -> 73.8 us
  waiting for transfers between devices: 141 us -> 148 us
  matrix products: 11.9 us -> 6.77 us
  other arithmetic: 11.2 us -> 6.59 us
  local copies, waits for them, and re-layouts: 41 us -> 44.9 us
    all_to_all x4 -> x1, blocking collectives: 115 us -> 10.7 us  [gather_all(): held = lax.all_to_all(spread, axis, 0, 0, tiled=True)]
    all_to_all x3 -> x4, waiting for transfers between devices: 54.6 us -> 87.3 us  [the longest x1 39.3 us: local(): o_rows = lax.all_to_all(o_send, PLANE, 0, 0, tiled=True)]
    all_to_all x2 -> x4, waiting for transfers between devices: 82 us -> 54.8 us  [gather_all(): held = lax.all_to_all(spread, axis, 0, 0, tiled=True)]
    all_to_all x2 -> x4, starting transfers between devices: 11.4 us -> 25.8 us  [gather_all(): held = lax.all_to_all(spread, axis, 0, 0, tiled=True)]
    all_to_all x0 -> x1, blocking collectives: none -> 11.8 us  [local(): lax.all_to_all(out_part, CROSS, 0, 0, tiled=True)]
    transpose x1 -> x6, local copies, waits for them, and re-layouts: 0.83 us -> 12.5 us  [the longest x1 4.27 us: local(): q_eff.reshape(own_width, planes, plane, q_width).transpose(2, 0, 1, 3)]
    ppermute x3, starting transfers between devices: 9.71 us -> 17.2 us  [group_gather(): other = lax.ppermute(held, axis, pairs)]
    convert_element_type x2 -> x1, other arithmetic: 5.71 us -> 0.02 us  [local(): (local_rows.astype(jnp.float32) + mixed_sum).astype(jnp.bfloat16)]
  transfers between devices with their start and end apart: 9 -> 12, of which waited for: 7 -> 10; matrix products, arithmetic and copies ran while one was open for 14% -> 13% of each run, Pallas kernels for 0% -> 0%
where the time goes in v3:
time: 305 us; the launch traced here: 303 us
  waiting for transfers between devices  148 us (49%)
  starting transfers between devices  73.8 us (24%)
  local copies, waits for them, and re-layouts  44.9 us (15%)
  blocking collectives  22.6 us (7%)
  matrix products  6.77 us (2%)
  other arithmetic  6.59 us (2%)
    all_to_all x4, waiting for transfers between devices, gather_all(): held = lax.all_to_all(spread, axis, 0, 0, tiled=True)  54.8 us
    all_to_all x1, waiting for transfers between devices, local(): o_rows = lax.all_to_all(o_send, PLANE, 0, 0, tiled=True)  39.3 us
    all_to_all x1, waiting for transfers between devices, local(): q_rows = lax.all_to_all(q_send, PLANE, 0, 0, tiled=True)  31.5 us
    all_to_all x4, starting transfers between devices, gather_all(): held = lax.all_to_all(spread, axis, 0, 0, tiled=True)  25.8 us
    ppermute x3, starting transfers between devices, group_gather(): other = lax.ppermute(held, axis, pairs)  17.2 us
    all_to_all x1, blocking collectives, local(): lax.all_to_all(out_part, CROSS, 0, 0, tiled=True)  11.8 us
    ppermute x1, starting transfers between devices, passed_along(): return lax.ppermute(value, axis, pairs)  11.2 us
    unnamed x33, local copies, waits for them, and re-layouts  11.1 us
  transfers between devices with their start and end apart: 12, of which 10 were waited for; matrix products, arithmetic and copies ran while one was open for 13% of the time, Pallas kernels for 0%

profile of v3, /device:TPU:1, one launch (start us, length us, event | category | flops | bytes accessed | tf_op | source)
XLA Modules:
  0.0 303.4 jit_solution(935919738339141972)
XLA Ops:
  1.0 10.7 %all_to_all.50 = bf16[4,1,321,128]{3,2,1,0:T(8,128)(2,1)S(1)} all-to-all(bf16[4,1,321,128]{3,2,1,0:T(8,128)(2,1)S(1)} %broadcast_in_dim.21), channel_id=1, replica_groups=mesh['section'=8,'tp_x'=4,'tp_z'=4,'tp_y'=4] {'tp_y'}, dimensions={0} | all-to-all | bytes 657408 | tf_op jit(solution)/shard_map/all_to_all | solution.py:53
  13.2 6.4 %all-to-all-start.1 = ((bf16[4,4,321,128]{3,1,2,0:T(4,128)(2,1)}), bf16[4,4,321,128]{3,1,2,0:T(4,128)(2,1)S(1)}, u32[]{:S(2)}, u32[]{:S(2)}) async-start(bf16[4,4,321,128]{3,1,2,0:T(4,128)(2,1)} %broadcast_in_dim.23), calls=%async_computation.1 | async-start | bytes 2629632 | tf_op jit(solution)/shard_map/all_to_all | solution.py:53
  21.2 29.5 %all-to-all-done.1 = bf16[4,4,321,128]{3,1,2,0:T(4,128)(2,1)S(1)} async-done(((bf16[4,4,321,128]{3,1,2,0:T(4,128)(2,1)}), bf16[4,4,321,128]{3,1,2,0:T(4,128)(2,1)S(1)}, u32[]{:S(2)}, u32[]{:S(2)}) %all-to-all-start.1) | async-done | bytes 1314848 | tf_op jit(solution)/shard_map/all_to_all | solution.py:53
  50.7 4.2 %all-to-all-start.4 = ((bf16[16,128,128]{1,2,0:T(8,128)(2,1)}), bf16[16,128,128]{1,2,0:T(8,128)(2,1)}, u32[]{:S(2)}, u32[]{:S(2)}) async-start(bf16[16,128,128]{1,2,0:T(8,128)(2,1)} %bitcast.11), calls=%async_computation.4 | async-start | bytes 1048576 | tf_op jit(solution)/shard_map/all_to_all | solution.py:108
  55.1 3.2 %copy.164 = bf16[1,128,8192]{1,2,0:T(8,128)(2,1)S(1)} copy(bf16[1,128,8192]{2,1,0:T(8,128)(2,1)} %param.14) | data formatting | bytes 4194304 | tf_op args[2]
  60.1 8.3 %all-to-all-done.4 = bf16[16,128,128]{1,2,0:T(8,128)(2,1)} async-done(((bf16[16,128,128]{1,2,0:T(8,128)(2,1)}), bf16[16,128,128]{1,2,0:T(8,128)(2,1)}, u32[]{:S(2)}, u32[]{:S(2)}) %all-to-all-start.4) | async-done | bytes 524320 | tf_op jit(solution)/shard_map/all_to_all | solution.py:108
  69.0 4.0 %all-to-all-start.2 = ((f32[4,1,320]{2,1,0:T(1,128)}), f32[4,1,320]{2,1,0:T(1,128)S(1)}, u32[]{:S(2)}, u32[]{:S(2)}) async-start(f32[4,1,320]{2,1,0:T(1,128)} %broadcast_in_dim.24), calls=%async_computation.2 | async-start | bytes 12288 | tf_op jit(solution)/shard_map/all_to_all | solution.py:53
  74.9 4.3 %copy.165 = bf16[16,128,4,128]{3,2,1,0:T(4,128)(2,1)} copy(bf16[16,128,4,128]{1,3,0,2:T(8,128)(2,1)} %fusion.5) | data formatting | bytes 4194304 | tf_op jit(solution)/shard_map/transpose | solution.py:102
  79.1 5.5 %all-to-all-start.3 = ((bf16[16,128,4,128]{3,2,1,0:T(4,128)(2,1)}), bf16[16,128,4,128]{3,2,1,0:T(4,128)(2,1)S(1)}, u32[]{:S(2)}, u32[]{:S(2)}) async-start(bf16[16,128,4,128]{3,2,1,0:T(4,128)(2,1)} %copy.165), calls=%async_computation.3 | async-start | bytes 4194304 | tf_op jit(solution)/shard_map/all_to_all | solution.py:103
  94.7 31.5 %all-to-all-done.3 = bf16[16,128,4,128]{3,2,1,0:T(4,128)(2,1)S(1)} async-done(((bf16[16,128,4,128]{3,2,1,0:T(4,128)(2,1)}), bf16[16,128,4,128]{3,2,1,0:T(4,128)(2,1)S(1)}, u32[]{:S(2)}, u32[]{:S(2)}) %all-to-all-start.3) | async-done | bytes 2097184 | tf_op jit(solution)/shard_map/all_to_all | solution.py:103
  133.5 4.2 %all-to-all-start.5 = ((f32[4,320,160]{1,2,0:T(8,128)}), f32[4,320,160]{1,2,0:T(8,128)S(1)}, u32[]{:S(2)}, u32[]{:S(2)}) async-start(f32[4,320,160]{1,2,0:T(8,128)} %copy.172), calls=%async_computation.5 | async-start | bytes 1966080 | tf_op jit(solution)/shard_map/all_to_all | solution.py:131
  137.8 3.2 %copy.186 = bf16[1,128,8192]{1,2,0:T(8,128)(2,1)S(1)} copy(bf16[1,128,8192]{2,1,0:T(8,128)(2,1)} %param.20) | data formatting | bytes 4194304 | tf_op args[8]
  141.1 8.2 %all-to-all-done.5 = f32[4,320,160]{1,2,0:T(8,128)S(1)} async-done(((f32[4,320,160]{1,2,0:T(8,128)}), f32[4,320,160]{1,2,0:T(8,128)S(1)}, u32[]{:S(2)}, u32[]{:S(2)}) %all-to-all-start.5) | async-done | bytes 819232 | tf_op jit(solution)/shard_map/all_to_all | solution.py:131
  154.4 5.9 %collective-permute-start.1 = (bf16[2,320,32]{1,2,0:T(8,128)(2,1)S(1)}, bf16[2,320,32]{1,2,0:T(8,128)(2,1)S(1)}, u32[]{:S(2)}, u32[]{:S(2)}) collective-permute-start(bf16[2,320,32]{1,2,0:T(8,128)(2,1)S(1)} %maximum_select_fusion.2), channel_id=1, source_target_pairs={{0,2},{1,3},{2,0},{3,1},{4,6},{5,7},{6,4},{7,5},{8,10},{9,11},{10,... | collective-permute-start | bytes 122888 | tf_op jit(solution)/shard_map/ppermute | solution.py:65
  162.1 8.8 %collective-permute-start.2 = (bf16[4,320,32]{1,2,0:T(8,128)(2,1)S(1)}, bf16[4,320,32]{1,2,0:T(8,128)(2,1)S(1)}, u32[]{:S(2)}, u32[]{:S(2)}) collective-permute-start(bf16[4,320,32]{1,2,0:T(8,128)(2,1)S(1)} %maximum_select_fusion.1), channel_id=1, source_target_pairs={{0,4},{1,5},{2,6},{3,7},{4,0},{5,1},{6,2},{7,3},{8,12},{9,13},{10,... | collective-permute-start | bytes 245768 | tf_op jit(solution)/shard_map/ppermute | solution.py:65
  174.5 4.2 %all-to-all-start.6 = ((bf16[4,1,320,128]{3,2,1,0:T(8,128)(2,1)}), bf16[4,1,320,128]{3,2,1,0:T(8,128)(2,1)S(1)}, u32[]{:S(2)}, u32[]{:S(2)}) async-start(bf16[4,1,320,128]{3,2,1,0:T(8,128)(2,1)} %broadcast_in_dim.28), calls=%async_computation.6 | async-start | bytes 655360 | tf_op jit(solution)/shard_map/all_to_all | solution.py:53
  180.5 4.3 %copy.187 = bf16[16,128,4,128]{3,2,1,0:T(4,128)(2,1)} copy(bf16[16,128,4,128]{1,3,0,2:T(8,128)(2,1)} %fusion.6) | data formatting | bytes 4194304 | tf_op jit(solution)/shard_map/transpose | solution.py:111
  184.8 5.5 %all-to-all-start.8 = ((bf16[16,128,4,128]{3,2,1,0:T(4,128)(2,1)}), bf16[16,128,4,128]{3,2,1,0:T(4,128)(2,1)S(1)}, u32[]{:S(2)}, u32[]{:S(2)}) async-start(bf16[16,128,4,128]{3,2,1,0:T(4,128)(2,1)} %copy.187), calls=%async_computation.8 | async-start | bytes 4194304 | tf_op jit(solution)/shard_map/all_to_all | solution.py:112
  190.5 39.3 %all-to-all-done.8 = bf16[16,128,4,128]{3,2,1,0:T(4,128)(2,1)S(1)} async-done(((bf16[16,128,4,128]{3,2,1,0:T(4,128)(2,1)}), bf16[16,128,4,128]{3,2,1,0:T(4,128)(2,1)S(1)}, u32[]{:S(2)}, u32[]{:S(2)}) %all-to-all-start.8) | async-done | bytes 2097184 | tf_op jit(solution)/shard_map/all_to_all | solution.py:112
  231.3 11.2 %all-to-all-start.7 = ((bf16[4,4,320,128]{3,1,2,0:T(4,128)(2,1)}), bf16[4,4,320,128]{3,1,2,0:T(4,128)(2,1)S(1)}, u32[]{:S(2)}, u32[]{:S(2)}) async-start(bf16[4,4,320,128]{3,1,2,0:T(4,128)(2,1)} %broadcast_in_dim.30), calls=%async_computation.7 | async-start | bytes 2621440 | tf_op jit(solution)/shard_map/all_to_all | solution.py:53
  244.2 3.9 %copy.188 = bf16[2048,512]{0,1:T(8,128)(2,1)} copy(bf16[2048,512]{1,0:T(8,128)(2,1)} %bitcast.98) | data formatting | bytes 4194304 | tf_op jit(solution)/shard_map/reshape | solution.py:113
  248.1 25.3 %all-to-all-done.7 = bf16[4,4,320,128]{3,1,2,0:T(4,128)(2,1)S(1)} async-done(((bf16[4,4,320,128]{3,1,2,0:T(4,128)(2,1)}), bf16[4,4,320,128]{3,1,2,0:T(4,128)(2,1)S(1)}, u32[]{:S(2)}, u32[]{:S(2)}) %all-to-all-start.7) | async-done | bytes 1310752 | tf_op jit(solution)/shard_map/all_to_all | solution.py:53
  278.2 11.8 %all_to_all.51 = f32[4,320,128]{2,1,0:T(8,128)S(1)} all-to-all(f32[4,320,128]{2,1,0:T(8,128)S(1)} %convolution_bitcast_fusion), channel_id=1, replica_groups=mesh['section'=8,'tp_x'=4,'tp_z'=4,'tp_y'=4] {'tp_x'}, dimensions={0} | all-to-all | bytes 1310720 | tf_op jit(solution)/shard_map/all_to_all | solution.py:157
  290.1 11.2 %collective-permute-start.3 = (bf16[320,128]{1,0:T(8,128)(2,1)S(1)}, bf16[320,128]{1,0:T(8,128)(2,1)S(1)}, u32[]{:S(2)}, u32[]{:S(2)}) collective-permute-start(bf16[320,128]{1,0:T(8,128)(2,1)S(1)} %add_convert_fusion), channel_id=1, source_target_pairs={{0,64},{64,128},{128,192},{192,256},{256,320},{320,384},{384,448},... | collective-permute-start | bytes 245768 | tf_op jit(solution)/shard_map/ppermute | solution.py:21
  (102 shorter events, 48.1 us)
Async XLA Ops:
  11.8 7.9 %copy-start.4 = (bf16[1,128,2048]{2,1,0:T(8,128)(2,1)S(1)}, bf16[1,128,2048]{2,1,0:T(8,128)(2,1)}, u32[]{:S(2)}) copy-start(bf16[1,128,2048]{2,1,0:T(8,128)(2,1)} %param.17) | copy-start | bytes 1572868
  13.2 6.8 %copy-start.11 = (f32[1,1,16]{2,1,0:T(1,128)S(1)}, f32[1,1,16]{2,1,0:T(1,128)}, u32[]{:S(2)}) copy-start(f32[1,1,16]{2,1,0:T(1,128)} %param.18) | copy-start | bytes 196
  13.2 6.8 %copy-start.12 = (s32[1,1,16]{2,1,0:T(1,128)S(1)}, s32[1,1,16]{2,1,0:T(1,128)}, u32[]{:S(2)}) copy-start(s32[1,1,16]{2,1,0:T(1,128)} %param.19) | copy-start | bytes 196
  13.2 37.4 %all-to-all-start.1 = ((bf16[4,4,321,128]{3,1,2,0:T(4,128)(2,1)}), bf16[4,4,321,128]{3,1,2,0:T(4,128)(2,1)S(1)}, u32[]{:S(2)}, u32[]{:S(2)}) async-start(bf16[4,4,321,128]{3,1,2,0:T(4,128)(2,1)} %broadcast_in_dim.23), calls=%async_computation.1 | async-start | bytes 2629632 | tf_op jit(solution)/shard_map/all_to_all | solution.py:53
  19.7 35.2 %copy-start.6 = (f32[1,1,64]{2,1,0:T(1,128)S(1)}, f32[1,1,64]{2,1,0:T(1,128)}, u32[]{:S(2)}) copy-start(f32[1,1,64]{2,1,0:T(1,128)} %param.21) | copy-start | bytes 772
  19.7 35.2 %copy-start.7 = (s32[1,1,64]{2,1,0:T(1,128)S(1)}, s32[1,1,64]{2,1,0:T(1,128)}, u32[]{:S(2)}) copy-start(s32[1,1,64]{2,1,0:T(1,128)} %param.22) | copy-start | bytes 772
  19.7 35.3 %copy-start.8 = (f32[1,1,64]{2,1,0:T(1,128)S(1)}, f32[1,1,64]{2,1,0:T(1,128)}, u32[]{:S(2)}) copy-start(f32[1,1,64]{2,1,0:T(1,128)} %param.15) | copy-start | bytes 772
  19.7 35.2 %copy-start.9 = (s32[1,1,64]{2,1,0:T(1,128)S(1)}, s32[1,1,64]{2,1,0:T(1,128)}, u32[]{:S(2)}) copy-start(s32[1,1,64]{2,1,0:T(1,128)} %param.16) | copy-start | bytes 772
  50.7 4.4 %copy-start = (bf16[4,4,321,128]{3,1,2,0:T(4,128)(2,1)}, bf16[4,4,321,128]{3,1,2,0:T(4,128)(2,1)S(1)}, u32[]{:S(2)}) copy-start(bf16[4,4,321,128]{3,1,2,0:T(4,128)(2,1)S(1)} %all-to-all-done.1) | copy-start | bytes 3944452
  50.7 17.8 %all-to-all-start.4 = ((bf16[16,128,128]{1,2,0:T(8,128)(2,1)}), bf16[16,128,128]{1,2,0:T(8,128)(2,1)}, u32[]{:S(2)}, u32[]{:S(2)}) async-start(bf16[16,128,128]{1,2,0:T(8,128)(2,1)} %bitcast.11), calls=%async_computation.4 | async-start | bytes 1048576 | tf_op jit(solution)/shard_map/all_to_all | solution.py:108
  69.0 10.1 %all-to-all-start.2 = ((f32[4,1,320]{2,1,0:T(1,128)}), f32[4,1,320]{2,1,0:T(1,128)S(1)}, u32[]{:S(2)}, u32[]{:S(2)}) async-start(f32[4,1,320]{2,1,0:T(1,128)} %broadcast_in_dim.24), calls=%async_computation.2 | async-start | bytes 12288 | tf_op jit(solution)/shard_map/all_to_all | solution.py:53
  79.1 47.0 %all-to-all-start.3 = ((bf16[16,128,4,128]{3,2,1,0:T(4,128)(2,1)}), bf16[16,128,4,128]{3,2,1,0:T(4,128)(2,1)S(1)}, u32[]{:S(2)}, u32[]{:S(2)}) async-start(bf16[16,128,4,128]{3,2,1,0:T(4,128)(2,1)} %copy.165), calls=%async_computation.3 | async-start | bytes 4194304 | tf_op jit(solution)/shard_map/all_to_all | solution.py:103
  127.9 3.0 %copy-start.2 = (bf16[320,2048,1]{1,0,2:T(8,128)(2,1)S(1)}, bf16[320,2048,1]{1,0,2:T(8,128)(2,1)}, u32[]{:S(2)}) copy-start(bf16[320,2048,1]{1,0,2:T(8,128)(2,1)} %reshape.482) | copy-start | bytes 3932164
  133.5 15.8 %all-to-all-start.5 = ((f32[4,320,160]{1,2,0:T(8,128)}), f32[4,320,160]{1,2,0:T(8,128)S(1)}, u32[]{:S(2)}, u32[]{:S(2)}) async-start(f32[4,320,160]{1,2,0:T(8,128)} %copy.172), calls=%async_computation.5 | async-start | bytes 1966080 | tf_op jit(solution)/shard_map/all_to_all | solution.py:131
  149.3 23.7 %copy-start.10 = (s32[320]{0:T(512)S(1)}, s32[320]{0:T(512)}, u32[]{:S(2)}) copy-start(s32[320]{0:T(512)} %param.23) | copy-start | bytes 3844
  149.9 4.6 %collective-permute-start = (bf16[1,320,32]{1,2,0:T(8,128)(2,1)S(1)}, bf16[1,320,32]{1,2,0:T(8,128)(2,1)S(1)}, u32[]{:S(2)}, u32[]{:S(2)}) collective-permute-start(bf16[1,320,32]{1,2,0:T(8,128)(2,1)S(1)} %pad_maximum_fusion.2), channel_id=1, source_target_pairs={{0,1},{1,0},{2,3},{3,2},{4,5},{5,4},{6,7},{7,6},{8,9},{9,8},{10,11... | collective-permute-start | bytes 61448 | tf_op jit(solution)/shard_map/ppermute | solution.py:65
  154.4 7.6 %collective-permute-start.1 = (bf16[2,320,32]{1,2,0:T(8,128)(2,1)S(1)}, bf16[2,320,32]{1,2,0:T(8,128)(2,1)S(1)}, u32[]{:S(2)}, u32[]{:S(2)}) collective-permute-start(bf16[2,320,32]{1,2,0:T(8,128)(2,1)S(1)} %maximum_select_fusion.2), channel_id=1, source_target_pairs={{0,2},{1,3},{2,0},{3,1},{4,6},{5,7},{6,4},{7,5},{8,10},{9,11},{10,... | collective-permute-start | bytes 122888 | tf_op jit(solution)/shard_map/ppermute | solution.py:65
  162.1 10.8 %collective-permute-start.2 = (bf16[4,320,32]{1,2,0:T(8,128)(2,1)S(1)}, bf16[4,320,32]{1,2,0:T(8,128)(2,1)S(1)}, u32[]{:S(2)}, u32[]{:S(2)}) collective-permute-start(bf16[4,320,32]{1,2,0:T(8,128)(2,1)S(1)} %maximum_select_fusion.1), channel_id=1, source_target_pairs={{0,4},{1,5},{2,6},{3,7},{4,0},{5,1},{6,2},{7,3},{8,12},{9,13},{10,... | collective-permute-start | bytes 245768 | tf_op jit(solution)/shard_map/ppermute | solution.py:65
  174.5 10.3 %all-to-all-start.6 = ((bf16[4,1,320,128]{3,2,1,0:T(8,128)(2,1)}), bf16[4,1,320,128]{3,2,1,0:T(8,128)(2,1)S(1)}, u32[]{:S(2)}, u32[]{:S(2)}) async-start(bf16[4,1,320,128]{3,2,1,0:T(8,128)(2,1)} %broadcast_in_dim.28), calls=%async_computation.6 | async-start | bytes 655360 | tf_op jit(solution)/shard_map/all_to_all | solution.py:53
  184.8 45.1 %all-to-all-start.8 = ((bf16[16,128,4,128]{3,2,1,0:T(4,128)(2,1)}), bf16[16,128,4,128]{3,2,1,0:T(4,128)(2,1)S(1)}, u32[]{:S(2)}, u32[]{:S(2)}) async-start(bf16[16,128,4,128]{3,2,1,0:T(4,128)(2,1)} %copy.187), calls=%async_computation.8 | async-start | bytes 4194304 | tf_op jit(solution)/shard_map/all_to_all | solution.py:112
  231.3 42.1 %all-to-all-start.7 = ((bf16[4,4,320,128]{3,1,2,0:T(4,128)(2,1)}), bf16[4,4,320,128]{3,1,2,0:T(4,128)(2,1)S(1)}, u32[]{:S(2)}, u32[]{:S(2)}) async-start(bf16[4,4,320,128]{3,1,2,0:T(4,128)(2,1)} %broadcast_in_dim.30), calls=%async_computation.7 | async-start | bytes 2621440 | tf_op jit(solution)/shard_map/all_to_all | solution.py:53
  273.7 2.3 copy-start.1
  278.2 11.9 %copy-start.5 = (bf16[1,320,128]{2,1,0:T(8,128)(2,1)S(1)}, bf16[1,320,128]{2,1,0:T(8,128)(2,1)}, u32[]{:S(2)}) copy-start(bf16[1,320,128]{2,1,0:T(8,128)(2,1)} %param.12) | copy-start | bytes 245764
  290.1 12.7 %collective-permute-start.3 = (bf16[320,128]{1,0:T(8,128)(2,1)S(1)}, bf16[320,128]{1,0:T(8,128)(2,1)S(1)}, u32[]{:S(2)}, u32[]{:S(2)}) collective-permute-start(bf16[320,128]{1,0:T(8,128)(2,1)S(1)} %add_convert_fusion), channel_id=1, source_target_pairs={{0,64},{64,128},{128,192},{192,256},{256,320},{320,384},{384,448},... | collective-permute-start | bytes 245768 | tf_op jit(solution)/shard_map/ppermute | solution.py:21
  (1 other events, 1.1 us)

commit v4 on v3

--- a/solution.py
+++ b/solution.py
@@ -134,7 +134,9 @@
     member = own_index % members
     key_part = rotate(summed[:, q_width : q_width + chunk], member * chunk)
     kv_part = jnp.concatenate([key_part, summed[:, q_width + chunk :]], axis=1).astype(jnp.bfloat16)
-    kv_group = group_gather(kv_part, TP_AXES, members)
+    plane_all = gather_all(kv_part, PLANE)
+    first = (lax.axis_index(PLANE) // members) * members
+    kv_group = lax.dynamic_slice_in_dim(plane_all, first, members, 0)
     key_rows = kv_group[:, :, :chunk].transpose(1, 0, 2).reshape(tok_count, HD)
     value_rows = kv_group[:, :, chunk:].transpose(1, 0, 2).reshape(tok_count, HD)
 

time: 305 us -> 308 us (level)
  starting transfers between devices: 73.8 us -> 63.4 us
  blocking collectives: 22.6 us -> 32.3 us
  waiting for transfers between devices: 148 us -> 152 us
    ppermute x3 -> x0, starting transfers between devices: 17.2 us -> none  [group_gather(): other = lax.ppermute(held, axis, pairs)]
    all_to_all x1 -> x2, blocking collectives: 10.7 us -> 20.4 us  [gather_all(): held = lax.all_to_all(spread, axis, 0, 0, tiled=True)]
    all_to_all x4 -> x5, starting transfers between devices: 25.8 us -> 32.2 us  [gather_all(): held = lax.all_to_all(spread, axis, 0, 0, tiled=True)]
    ppermute x3 -> x0, waiting for transfers between devices: 4.81 us -> none  [group_gather(): other = lax.ppermute(held, axis, pairs)]
    all_to_all x4 -> x5, waiting for transfers between devices: 54.8 us -> 58.2 us  [gather_all(): held = lax.all_to_all(spread, axis, 0, 0, tiled=True)]
    all_to_all x1, waiting for transfers between devices: 8.17 us -> 11.5 us  [local(): summed = jnp.sum(lax.all_to_all(packed, CROSS, 0, 0, tiled=True), axis=0)]
  transfers between devices with their start and end apart: 12 -> 10, of which waited for: 10 -> 8; matrix products, arithmetic and copies ran while one was open for 13% -> 13% of each run, Pallas kernels for 0% -> 0%
where the time goes in v4:
time: 308 us; the launch traced here: 307 us
  waiting for transfers between devices  152 us (49%)
  starting transfers between devices  63.4 us (21%)
  local copies, waits for them, and re-layouts  45.6 us (15%)
  blocking collectives  32.3 us (10%)
  matrix products  6.77 us (2%)
  other arithmetic  6.46 us (2%)
    all_to_all x5, waiting for transfers between devices, gather_all(): held = lax.all_to_all(spread, axis, 0, 0, tiled=True)  58.2 us
    all_to_all x1, waiting for transfers between devices, local(): o_rows = lax.all_to_all(o_send, PLANE, 0, 0, tiled=True)  40.7 us
    all_to_all x5, starting transfers between devices, gather_all(): held = lax.all_to_all(spread, axis, 0, 0, tiled=True)  32.2 us
    all_to_all x1, waiting for transfers between devices, local(): q_rows = lax.all_to_all(q_send, PLANE, 0, 0, tiled=True)  31.5 us
    all_to_all x2, blocking collectives, gather_all(): held = lax.all_to_all(spread, axis, 0, 0, tiled=True)  20.4 us
    all_to_all x1, blocking collectives, local(): lax.all_to_all(out_part, CROSS, 0, 0, tiled=True)  11.8 us
    all_to_all x1, waiting for transfers between devices, local(): summed = jnp.sum(lax.all_to_all(packed, CROSS, 0, 0, tiled=True), axis=0)  11.5 us
    ppermute x1, starting transfers between devices, passed_along(): return lax.ppermute(value, axis, pairs)  11.2 us
  transfers between devices with their start and end apart: 10, of which 8 were waited for; matrix products, arithmetic and copies ran while one was open for 13% of the time, Pallas kernels for 0%

profile of v4, /device:TPU:1, one launch (start us, length us, event | category | flops | bytes accessed | tf_op | source)
XLA Modules:
  0.0 306.6 jit_solution(7067863524978501981)
XLA Ops:
  1.0 10.7 %all_to_all.60 = bf16[4,1,321,128]{3,2,1,0:T(8,128)(2,1)S(1)} all-to-all(bf16[4,1,321,128]{3,2,1,0:T(8,128)(2,1)S(1)} %broadcast_in_dim.27), channel_id=1, replica_groups=mesh['section'=8,'tp_x'=4,'tp_z'=4,'tp_y'=4] {'tp_y'}, dimensions={0} | all-to-all | bytes 657408 | tf_op jit(solution)/shard_map/all_to_all | solution.py:53
  13.2 6.4 %all-to-all-start.1 = ((bf16[4,4,321,128]{3,1,2,0:T(4,128)(2,1)}), bf16[4,4,321,128]{3,1,2,0:T(4,128)(2,1)S(1)}, u32[]{:S(2)}, u32[]{:S(2)}) async-start(bf16[4,4,321,128]{3,1,2,0:T(4,128)(2,1)} %broadcast_in_dim.29), calls=%async_computation.1 | async-start | bytes 2629632 | tf_op jit(solution)/shard_map/all_to_all | solution.py:53
  21.2 29.5 %all-to-all-done.1 = bf16[4,4,321,128]{3,1,2,0:T(4,128)(2,1)S(1)} async-done(((bf16[4,4,321,128]{3,1,2,0:T(4,128)(2,1)}), bf16[4,4,321,128]{3,1,2,0:T(4,128)(2,1)S(1)}, u32[]{:S(2)}, u32[]{:S(2)}) %all-to-all-start.1) | async-done | bytes 1314848 | tf_op jit(solution)/shard_map/all_to_all | solution.py:53
  50.7 4.2 %all-to-all-start.4 = ((bf16[16,128,128]{1,2,0:T(8,128)(2,1)}), bf16[16,128,128]{1,2,0:T(8,128)(2,1)}, u32[]{:S(2)}, u32[]{:S(2)}) async-start(bf16[16,128,128]{1,2,0:T(8,128)(2,1)} %bitcast.11), calls=%async_computation.4 | async-start | bytes 1048576 | tf_op jit(solution)/shard_map/all_to_all | solution.py:108
  55.1 3.2 %copy.161 = bf16[1,128,8192]{1,2,0:T(8,128)(2,1)S(1)} copy(bf16[1,128,8192]{2,1,0:T(8,128)(2,1)} %param.14) | data formatting | bytes 4194304 | tf_op args[2]
  60.1 8.3 %all-to-all-done.4 = bf16[16,128,128]{1,2,0:T(8,128)(2,1)} async-done(((bf16[16,128,128]{1,2,0:T(8,128)(2,1)}), bf16[16,128,128]{1,2,0:T(8,128)(2,1)}, u32[]{:S(2)}, u32[]{:S(2)}) %all-to-all-start.4) | async-done | bytes 524320 | tf_op jit(solution)/shard_map/all_to_all | solution.py:108
  69.0 4.0 %all-to-all-start.2 = ((f32[4,1,320]{2,1,0:T(1,128)}), f32[4,1,320]{2,1,0:T(1,128)S(1)}, u32[]{:S(2)}, u32[]{:S(2)}) async-start(f32[4,1,320]{2,1,0:T(1,128)} %broadcast_in_dim.31), calls=%async_computation.2 | async-start | bytes 12288 | tf_op jit(solution)/shard_map/all_to_all | solution.py:53
  74.8 4.3 %copy.162 = bf16[16,128,4,128]{3,2,1,0:T(4,128)(2,1)} copy(bf16[16,128,4,128]{1,3,0,2:T(8,128)(2,1)} %fusion.5) | data formatting | bytes 4194304 | tf_op jit(solution)/shard_map/transpose | solution.py:102
  79.1 5.5 %all-to-all-start.3 = ((bf16[16,128,4,128]{3,2,1,0:T(4,128)(2,1)}), bf16[16,128,4,128]{3,2,1,0:T(4,128)(2,1)S(1)}, u32[]{:S(2)}, u32[]{:S(2)}) async-start(bf16[16,128,4,128]{3,2,1,0:T(4,128)(2,1)} %copy.162), calls=%async_computation.3 | async-start | bytes 4194304 | tf_op jit(solution)/shard_map/all_to_all | solution.py:103
  94.6 31.5 %all-to-all-done.3 = bf16[16,128,4,128]{3,2,1,0:T(4,128)(2,1)S(1)} async-done(((bf16[16,128,4,128]{3,2,1,0:T(4,128)(2,1)}), bf16[16,128,4,128]{3,2,1,0:T(4,128)(2,1)S(1)}, u32[]{:S(2)}, u32[]{:S(2)}) %all-to-all-start.3) | async-done | bytes 2097184 | tf_op jit(solution)/shard_map/all_to_all | solution.py:103
  133.4 4.2 %all-to-all-start.5 = ((f32[4,320,160]{1,2,0:T(8,128)}), f32[4,320,160]{1,2,0:T(8,128)S(1)}, u32[]{:S(2)}, u32[]{:S(2)}) async-start(f32[4,320,160]{1,2,0:T(8,128)} %copy.169), calls=%async_computation.5 | async-start | bytes 1966080 | tf_op jit(solution)/shard_map/all_to_all | solution.py:131
  137.7 11.5 %all-to-all-done.5 = f32[4,320,160]{1,2,0:T(8,128)S(1)} async-done(((f32[4,320,160]{1,2,0:T(8,128)}), f32[4,320,160]{1,2,0:T(8,128)S(1)}, u32[]{:S(2)}, u32[]{:S(2)}) %all-to-all-start.5) | async-done | bytes 819232 | tf_op jit(solution)/shard_map/all_to_all | solution.py:131
  149.8 9.7 %all_to_all.61 = bf16[4,1,320,32]{2,3,1,0:T(8,128)(2,1)S(1)} all-to-all(bf16[4,1,320,32]{2,3,1,0:T(8,128)(2,1)S(1)} %broadcast_in_dim.32), channel_id=1, replica_groups=mesh['section'=8,'tp_x'=4,'tp_z'=4,'tp_y'=4] {'tp_y'}, dimensions={0} | all-to-all | bytes 163840 | tf_op jit(solution)/shard_map/all_to_all | solution.py:53
  160.3 8.5 %all-to-all-start.7 = ((bf16[4,4,320,32]{2,3,1,0:T(8,128)(2,1)}), bf16[4,4,320,32]{2,3,1,0:T(8,128)(2,1)S(1)}, u32[]{:S(2)}, u32[]{:S(2)}) async-start(bf16[4,4,320,32]{2,3,1,0:T(8,128)(2,1)} %broadcast_in_dim.34), calls=%async_computation.7 | async-start | bytes 786432 | tf_op jit(solution)/shard_map/all_to_all | solution.py:53
  173.1 3.4 %all-to-all-done.7 = bf16[4,4,320,32]{2,3,1,0:T(8,128)(2,1)S(1)} async-done(((bf16[4,4,320,32]{2,3,1,0:T(8,128)(2,1)}), bf16[4,4,320,32]{2,3,1,0:T(8,128)(2,1)S(1)}, u32[]{:S(2)}, u32[]{:S(2)}) %all-to-all-start.7) | async-done | bytes 327712 | tf_op jit(solution)/shard_map/all_to_all | solution.py:53
  177.9 3.5 %all-to-all-start.8 = ((bf16[4,1,320,128]{3,2,1,0:T(8,128)(2,1)}), bf16[4,1,320,128]{3,2,1,0:T(8,128)(2,1)S(1)}, u32[]{:S(2)}, u32[]{:S(2)}) async-start(bf16[4,1,320,128]{3,2,1,0:T(8,128)(2,1)} %broadcast_in_dim.37), calls=%async_computation.8 | async-start | bytes 655360 | tf_op jit(solution)/shard_map/all_to_all | solution.py:53
  183.2 4.3 %copy.184 = bf16[16,128,4,128]{3,2,1,0:T(4,128)(2,1)} copy(bf16[16,128,4,128]{1,3,0,2:T(8,128)(2,1)} %fusion.6) | data formatting | bytes 4194304 | tf_op jit(solution)/shard_map/transpose | solution.py:111
  187.4 6.0 %all-to-all-start.10 = ((bf16[16,128,4,128]{3,2,1,0:T(4,128)(2,1)}), bf16[16,128,4,128]{3,2,1,0:T(4,128)(2,1)S(1)}, u32[]{:S(2)}, u32[]{:S(2)}) async-start(bf16[16,128,4,128]{3,2,1,0:T(4,128)(2,1)} %copy.184), calls=%async_computation.10 | async-start | bytes 4194304 | tf_op jit(solution)/shard_map/all_to_all | solution.py:112
  193.7 40.7 %all-to-all-done.10 = bf16[16,128,4,128]{3,2,1,0:T(4,128)(2,1)S(1)} async-done(((bf16[16,128,4,128]{3,2,1,0:T(4,128)(2,1)}), bf16[16,128,4,128]{3,2,1,0:T(4,128)(2,1)S(1)}, u32[]{:S(2)}, u32[]{:S(2)}) %all-to-all-start.10) | async-done | bytes 2097184 | tf_op jit(solution)/shard_map/all_to_all | solution.py:112
  235.9 9.8 %all-to-all-start.9 = ((bf16[4,4,320,128]{3,1,2,0:T(4,128)(2,1)}), bf16[4,4,320,128]{3,1,2,0:T(4,128)(2,1)S(1)}, u32[]{:S(2)}, u32[]{:S(2)}) async-start(bf16[4,4,320,128]{3,1,2,0:T(4,128)(2,1)} %broadcast_in_dim.76), calls=%async_computation.9 | async-start | bytes 2621440 | tf_op jit(solution)/shard_map/all_to_all | solution.py:53
  247.4 4.0 %copy.185 = bf16[2048,512]{0,1:T(8,128)(2,1)} copy(bf16[2048,512]{1,0:T(8,128)(2,1)} %bitcast.97) | data formatting | bytes 4194304 | tf_op jit(solution)/shard_map/reshape | solution.py:113
  251.3 25.3 %all-to-all-done.9 = bf16[4,4,320,128]{3,1,2,0:T(4,128)(2,1)S(1)} async-done(((bf16[4,4,320,128]{3,1,2,0:T(4,128)(2,1)}), bf16[4,4,320,128]{3,1,2,0:T(4,128)(2,1)S(1)}, u32[]{:S(2)}, u32[]{:S(2)}) %all-to-all-start.9) | async-done | bytes 1310752 | tf_op jit(solution)/shard_map/all_to_all | solution.py:53
  281.4 11.8 %all_to_all.62 = f32[4,320,128]{2,1,0:T(8,128)S(1)} all-to-all(f32[4,320,128]{2,1,0:T(8,128)S(1)} %convolution_bitcast_fusion), channel_id=1, replica_groups=mesh['section'=8,'tp_x'=4,'tp_z'=4,'tp_y'=4] {'tp_x'}, dimensions={0} | all-to-all | bytes 1310720 | tf_op jit(solution)/shard_map/all_to_all | solution.py:159
  293.3 11.2 %collective-permute-start = (bf16[320,128]{1,0:T(8,128)(2,1)S(1)}, bf16[320,128]{1,0:T(8,128)(2,1)S(1)}, u32[]{:S(2)}, u32[]{:S(2)}) collective-permute-start(bf16[320,128]{1,0:T(8,128)(2,1)S(1)} %add_convert_fusion), channel_id=1, source_target_pairs={{0,64},{64,128},{128,192},{192,256},{256,320},{320,384},{384,448},... | collective-permute-start | bytes 245768 | tf_op jit(solution)/shard_map/ppermute | solution.py:21
  (98 shorter events, 44.6 us)
Async XLA Ops:
  11.8 7.9 %copy-start.4 = (bf16[1,128,2048]{2,1,0:T(8,128)(2,1)S(1)}, bf16[1,128,2048]{2,1,0:T(8,128)(2,1)}, u32[]{:S(2)}) copy-start(bf16[1,128,2048]{2,1,0:T(8,128)(2,1)} %param.17) | copy-start | bytes 1572868
  13.2 6.8 %copy-start.11 = (f32[1,1,16]{2,1,0:T(1,128)S(1)}, f32[1,1,16]{2,1,0:T(1,128)}, u32[]{:S(2)}) copy-start(f32[1,1,16]{2,1,0:T(1,128)} %param.18) | copy-start | bytes 196
  13.2 6.8 %copy-start.12 = (s32[1,1,16]{2,1,0:T(1,128)S(1)}, s32[1,1,16]{2,1,0:T(1,128)}, u32[]{:S(2)}) copy-start(s32[1,1,16]{2,1,0:T(1,128)} %param.19) | copy-start | bytes 196
  13.2 37.4 %all-to-all-start.1 = ((bf16[4,4,321,128]{3,1,2,0:T(4,128)(2,1)}), bf16[4,4,321,128]{3,1,2,0:T(4,128)(2,1)S(1)}, u32[]{:S(2)}, u32[]{:S(2)}) async-start(bf16[4,4,321,128]{3,1,2,0:T(4,128)(2,1)} %broadcast_in_dim.29), calls=%async_computation.1 | async-start | bytes 2629632 | tf_op jit(solution)/shard_map/all_to_all | solution.py:53
  19.7 35.2 %copy-start.6 = (f32[1,1,64]{2,1,0:T(1,128)S(1)}, f32[1,1,64]{2,1,0:T(1,128)}, u32[]{:S(2)}) copy-start(f32[1,1,64]{2,1,0:T(1,128)} %param.21) | copy-start | bytes 772
  19.7 35.2 %copy-start.7 = (s32[1,1,64]{2,1,0:T(1,128)S(1)}, s32[1,1,64]{2,1,0:T(1,128)}, u32[]{:S(2)}) copy-start(s32[1,1,64]{2,1,0:T(1,128)} %param.22) | copy-start | bytes 772
  19.7 35.2 %copy-start.8 = (f32[1,1,64]{2,1,0:T(1,128)S(1)}, f32[1,1,64]{2,1,0:T(1,128)}, u32[]{:S(2)}) copy-start(f32[1,1,64]{2,1,0:T(1,128)} %param.15) | copy-start | bytes 772
  19.7 35.2 %copy-start.9 = (s32[1,1,64]{2,1,0:T(1,128)S(1)}, s32[1,1,64]{2,1,0:T(1,128)}, u32[]{:S(2)}) copy-start(s32[1,1,64]{2,1,0:T(1,128)} %param.16) | copy-start | bytes 772
  50.7 4.4 %copy-start = (bf16[4,4,321,128]{3,1,2,0:T(4,128)(2,1)}, bf16[4,4,321,128]{3,1,2,0:T(4,128)(2,1)S(1)}, u32[]{:S(2)}) copy-start(bf16[4,4,321,128]{3,1,2,0:T(4,128)(2,1)S(1)} %all-to-all-done.1) | copy-start | bytes 3944452
  50.7 17.8 %all-to-all-start.4 = ((bf16[16,128,128]{1,2,0:T(8,128)(2,1)}), bf16[16,128,128]{1,2,0:T(8,128)(2,1)}, u32[]{:S(2)}, u32[]{:S(2)}) async-start(bf16[16,128,128]{1,2,0:T(8,128)(2,1)} %bitcast.11), calls=%async_computation.4 | async-start | bytes 1048576 | tf_op jit(solution)/shard_map/all_to_all | solution.py:108
  69.0 10.1 %all-to-all-start.2 = ((f32[4,1,320]{2,1,0:T(1,128)}), f32[4,1,320]{2,1,0:T(1,128)S(1)}, u32[]{:S(2)}, u32[]{:S(2)}) async-start(f32[4,1,320]{2,1,0:T(1,128)} %broadcast_in_dim.31), calls=%async_computation.2 | async-start | bytes 12288 | tf_op jit(solution)/shard_map/all_to_all | solution.py:53
  79.1 47.0 %all-to-all-start.3 = ((bf16[16,128,4,128]{3,2,1,0:T(4,128)(2,1)}), bf16[16,128,4,128]{3,2,1,0:T(4,128)(2,1)S(1)}, u32[]{:S(2)}, u32[]{:S(2)}) async-start(bf16[16,128,4,128]{3,2,1,0:T(4,128)(2,1)} %copy.162), calls=%async_computation.3 | async-start | bytes 4194304 | tf_op jit(solution)/shard_map/all_to_all | solution.py:103
  127.8 3.0 copy-start.2
  130.9 1.1 copy-start.3
  133.4 15.8 %all-to-all-start.5 = ((f32[4,320,160]{1,2,0:T(8,128)}), f32[4,320,160]{1,2,0:T(8,128)S(1)}, u32[]{:S(2)}, u32[]{:S(2)}) async-start(f32[4,320,160]{1,2,0:T(8,128)} %copy.169), calls=%async_computation.5 | async-start | bytes 1966080 | tf_op jit(solution)/shard_map/all_to_all | solution.py:131
  160.3 16.2 %all-to-all-start.7 = ((bf16[4,4,320,32]{2,3,1,0:T(8,128)(2,1)}), bf16[4,4,320,32]{2,3,1,0:T(8,128)(2,1)S(1)}, u32[]{:S(2)}, u32[]{:S(2)}) async-start(bf16[4,4,320,32]{2,3,1,0:T(8,128)(2,1)} %broadcast_in_dim.34), calls=%async_computation.7 | async-start | bytes 786432 | tf_op jit(solution)/shard_map/all_to_all | solution.py:53
  172.1 4.5 %copy-start.10 = (s32[320]{0:T(512)S(1)}, s32[320]{0:T(512)}, u32[]{:S(2)}) copy-start(s32[320]{0:T(512)} %param.23) | copy-start | bytes 3844
  177.9 9.5 %all-to-all-start.8 = ((bf16[4,1,320,128]{3,2,1,0:T(8,128)(2,1)}), bf16[4,1,320,128]{3,2,1,0:T(8,128)(2,1)S(1)}, u32[]{:S(2)}, u32[]{:S(2)}) async-start(bf16[4,1,320,128]{3,2,1,0:T(8,128)(2,1)} %broadcast_in_dim.37), calls=%async_computation.8 | async-start | bytes 655360 | tf_op jit(solution)/shard_map/all_to_all | solution.py:53
  187.4 47.0 %all-to-all-start.10 = ((bf16[16,128,4,128]{3,2,1,0:T(4,128)(2,1)}), bf16[16,128,4,128]{3,2,1,0:T(4,128)(2,1)S(1)}, u32[]{:S(2)}, u32[]{:S(2)}) async-start(bf16[16,128,4,128]{3,2,1,0:T(4,128)(2,1)} %copy.184), calls=%async_computation.10 | async-start | bytes 4194304 | tf_op jit(solution)/shard_map/all_to_all | solution.py:112
  235.9 40.8 %all-to-all-start.9 = ((bf16[4,4,320,128]{3,1,2,0:T(4,128)(2,1)}), bf16[4,4,320,128]{3,1,2,0:T(4,128)(2,1)S(1)}, u32[]{:S(2)}, u32[]{:S(2)}) async-start(bf16[4,4,320,128]{3,1,2,0:T(4,128)(2,1)} %broadcast_in_dim.76), calls=%async_computation.9 | async-start | bytes 2621440 | tf_op jit(solution)/shard_map/all_to_all | solution.py:53
  276.9 2.3 copy-start.1
  281.4 11.9 %copy-start.5 = (bf16[1,320,128]{2,1,0:T(8,128)(2,1)S(1)}, bf16[1,320,128]{2,1,0:T(8,128)(2,1)}, u32[]{:S(2)}) copy-start(bf16[1,320,128]{2,1,0:T(8,128)(2,1)} %param.12) | copy-start | bytes 245764
  293.3 12.7 %collective-permute-start = (bf16[320,128]{1,0:T(8,128)(2,1)S(1)}, bf16[320,128]{1,0:T(8,128)(2,1)S(1)}, u32[]{:S(2)}, u32[]{:S(2)}) collective-permute-start(bf16[320,128]{1,0:T(8,128)(2,1)S(1)} %add_convert_fusion), channel_id=1, source_target_pairs={{0,64},{64,128},{128,192},{192,256},{256,320},{320,384},{384,448},... | collective-permute-start | bytes 245768 | tf_op jit(solution)/shard_map/ppermute | solution.py:21

commit v5 on v3

--- a/solution.py
+++ b/solution.py
@@ -100,13 +100,14 @@
 
     q_eff = dequant(query_weight[0], query_scale[0], query_keep[0])
     q_send = q_eff.reshape(own_width, planes, plane, q_width).transpose(2, 0, 1, 3)
-    q_rows = lax.all_to_all(q_send, PLANE, 0, 0, tiled=True)
-    q_rows = q_rows.reshape(plane * own_width, planes * q_width)
+    q_send = q_send.reshape(plane, own_width, planes * q_width)
     kv_eff = dequant(kv_weight[0], kv_scale[0], kv_keep[0])
     kv_send = kv_eff.reshape(own_width, 2, planes, halves, members, chunk)
     kv_send = kv_send.transpose(3, 4, 0, 2, 1, 5).reshape(plane, own_width, planes * 2 * chunk)
-    kv_rows = lax.all_to_all(kv_send, PLANE, 0, 0, tiled=True)
-    kv_rows = kv_rows.reshape(plane * own_width, planes * 2 * chunk)
+    both = jnp.concatenate([q_send, kv_send], axis=2)
+    both = lax.all_to_all(both, PLANE, 0, 0, tiled=True).reshape(plane * own_width, -1)
+    q_rows = both[:, : planes * q_width]
+    kv_rows = both[:, planes * q_width :]
     o_eff = dequant(out_weight[0], out_scale[0], out_keep[0])
     o_send = o_eff.reshape(q_width, planes, plane, own_width).transpose(2, 0, 1, 3)
     o_rows = lax.all_to_all(o_send, PLANE, 0, 0, tiled=True)

time: 305 us -> 302 us (level)
  waiting for transfers between devices: 148 us -> 154 us
  local copies, waits for them, and re-layouts: 44.9 us -> 39.6 us
  starting transfers between devices: 73.8 us -> 69.9 us
    all_to_all x2 -> x1, waiting for transfers between devices: 39.8 us -> 47.8 us  [local(): lax.all_to_all(both, PLANE, 0, 0, tiled=True).reshape(plane * own_width, -1)]
    all_to_all x2 -> x1, starting transfers between devices: 9.74 us -> 4.46 us  [local(): lax.all_to_all(both, PLANE, 0, 0, tiled=True).reshape(plane * own_width, -1)]
    dot_general x0 -> x2, local copies, waits for them, and re-layouts: none -> 4.42 us  [local(): q_part = jnp.dot(normed_pl, q_rows, preferred_element_type=jnp.float32)]
    transpose x1, local copies, waits for them, and re-layouts: 4.27 us -> 0.24 us  [local(): q_eff.reshape(own_width, planes, plane, q_width).transpose(2, 0, 1, 3)]
    unnamed x33 -> x28, local copies, waits for them, and re-layouts: 11.1 us -> 9.21 us
  transfers between devices with their start and end apart: 12 -> 11, of which waited for: 10 -> 10; matrix products, arithmetic and copies ran while one was open for 13% -> 9% of each run, Pallas kernels for 0% -> 0%
where the time goes in v5:
time: 302 us; the launch traced here: 301 us
  waiting for transfers between devices  154 us (51%)
  starting transfers between devices  69.9 us (23%)
  local copies, waits for them, and re-layouts  39.6 us (13%)
  blocking collectives  22.6 us (7%)
  other arithmetic  8 us (3%)
  matrix products  5.92 us (2%)
    all_to_all x4, waiting for transfers between devices, gather_all(): held = lax.all_to_all(spread, axis, 0, 0, tiled=True)  52.3 us
    all_to_all x1, waiting for transfers between devices, local(): lax.all_to_all(both, PLANE, 0, 0, tiled=True).reshape(plane * own_width, -1)  47.8 us
    all_to_all x1, waiting for transfers between devices, local(): o_rows = lax.all_to_all(o_send, PLANE, 0, 0, tiled=True)  39.6 us
    all_to_all x4, starting transfers between devices, gather_all(): held = lax.all_to_all(spread, axis, 0, 0, tiled=True)  25.6 us
    ppermute x3, starting transfers between devices, group_gather(): other = lax.ppermute(held, axis, pairs)  19.6 us
    all_to_all x1, blocking collectives, local(): lax.all_to_all(out_part, CROSS, 0, 0, tiled=True)  11.8 us
    ppermute x1, starting transfers between devices, passed_along(): return lax.ppermute(value, axis, pairs)  11.2 us
    all_to_all x1, blocking collectives, gather_all(): held = lax.all_to_all(spread, axis, 0, 0, tiled=True)  10.7 us
  transfers between devices with their start and end apart: 11, of which 10 were waited for; matrix products, arithmetic and copies ran while one was open for 9% of the time, Pallas kernels for 0%

profile of v5, /device:TPU:1, one launch (start us, length us, event | category | flops | bytes accessed | tf_op | source)
XLA Modules:
  0.0 300.8 jit_solution(3566516453952617379)
XLA Ops:
  1.0 10.7 %all_to_all.45 = bf16[4,1,321,128]{3,2,1,0:T(8,128)(2,1)S(1)} all-to-all(bf16[4,1,321,128]{3,2,1,0:T(8,128)(2,1)S(1)} %broadcast_in_dim.21), channel_id=1, replica_groups=mesh['section'=8,'tp_x'=4,'tp_z'=4,'tp_y'=4] {'tp_y'}, dimensions={0} | all-to-all | bytes 657408 | tf_op jit(solution)/shard_map/all_to_all | solution.py:53
  13.3 6.3 %all-to-all-start.1 = ((bf16[4,4,321,128]{3,1,2,0:T(4,128)(2,1)}), bf16[4,4,321,128]{3,1,2,0:T(4,128)(2,1)}, u32[]{:S(2)}, u32[]{:S(2)}) async-start(bf16[4,4,321,128]{3,1,2,0:T(4,128)(2,1)} %broadcast_in_dim.23), calls=%async_computation.1 | async-start | bytes 2629632 | tf_op jit(solution)/shard_map/all_to_all | solution.py:53
  21.2 3.2 %copy.166 = bf16[1,128,8192]{1,2,0:T(8,128)(2,1)S(1)} copy(bf16[1,128,8192]{2,1,0:T(8,128)(2,1)} %param.14) | data formatting | bytes 4194304 | tf_op args[2]
  25.1 25.6 %all-to-all-done.1 = bf16[4,4,321,128]{3,1,2,0:T(4,128)(2,1)} async-done(((bf16[4,4,321,128]{3,1,2,0:T(4,128)(2,1)}), bf16[4,4,321,128]{3,1,2,0:T(4,128)(2,1)}, u32[]{:S(2)}, u32[]{:S(2)}) %all-to-all-start.1) | async-done | bytes 1314848 | tf_op jit(solution)/shard_map/all_to_all | solution.py:53
  53.1 4.0 %all-to-all-start.2 = ((f32[4,1,320]{2,1,0:T(1,128)}), f32[4,1,320]{2,1,0:T(1,128)S(1)}, u32[]{:S(2)}, u32[]{:S(2)}) async-start(f32[4,1,320]{2,1,0:T(1,128)} %broadcast_in_dim.24), calls=%async_computation.2 | async-start | bytes 12288 | tf_op jit(solution)/shard_map/all_to_all | solution.py:53
  57.2 2.8 pad_maximum_fusion
  61.3 4.5 %all-to-all-start.3 = ((bf16[16,128,640]{1,2,0:T(8,128)(2,1)}), bf16[16,128,640]{1,2,0:T(8,128)(2,1)}, u32[]{:S(2)}, u32[]{:S(2)}) async-start(bf16[16,128,640]{1,2,0:T(8,128)(2,1)} %pad_maximum_fusion), calls=%async_computation.3 | async-start | bytes 5242880 | tf_op jit(solution)/shard_map/all_to_all | solution.py:108
  68.6 47.8 %all-to-all-done.3 = bf16[16,128,640]{1,2,0:T(8,128)(2,1)} async-done(((bf16[16,128,640]{1,2,0:T(8,128)(2,1)}), bf16[16,128,640]{1,2,0:T(8,128)(2,1)}, u32[]{:S(2)}, u32[]{:S(2)}) %all-to-all-start.3) | async-done | bytes 2621472 | tf_op jit(solution)/shard_map/all_to_all | solution.py:108
  116.4 3.1 %copy.170 = bf16[16,128,640]{2,1,0:T(8,128)(2,1)S(1)} copy(bf16[16,128,640]{1,2,0:T(8,128)(2,1)} %all-to-all-done.3) | data formatting | bytes 5242880 | tf_op jit(solution)/shard_map/all_to_all | solution.py:108
  121.1 2.9 copy.171
  128.9 3.5 %all-to-all-start.4 = ((f32[4,320,160]{1,2,0:T(8,128)}), f32[4,320,160]{1,2,0:T(8,128)S(1)}, u32[]{:S(2)}, u32[]{:S(2)}) async-start(f32[4,320,160]{1,2,0:T(8,128)} %copy.174), calls=%async_computation.4 | async-start | bytes 1966080 | tf_op jit(solution)/shard_map/all_to_all | solution.py:132
  132.5 3.2 %copy.188 = bf16[1,128,8192]{1,2,0:T(8,128)(2,1)S(1)} copy(bf16[1,128,8192]{2,1,0:T(8,128)(2,1)} %param.20) | data formatting | bytes 4194304 | tf_op args[8]
  135.8 8.1 %all-to-all-done.4 = f32[4,320,160]{1,2,0:T(8,128)S(1)} async-done(((f32[4,320,160]{1,2,0:T(8,128)}), f32[4,320,160]{1,2,0:T(8,128)S(1)}, u32[]{:S(2)}, u32[]{:S(2)}) %all-to-all-start.4) | async-done | bytes 819232 | tf_op jit(solution)/shard_map/all_to_all | solution.py:132
  149.2 7.0 %collective-permute-start.1 = (bf16[2,320,32]{1,2,0:T(8,128)(2,1)S(1)}, bf16[2,320,32]{1,2,0:T(8,128)(2,1)S(1)}, u32[]{:S(2)}, u32[]{:S(2)}) collective-permute-start(bf16[2,320,32]{1,2,0:T(8,128)(2,1)S(1)} %maximum_select_fusion.2), channel_id=1, source_target_pairs={{0,2},{1,3},{2,0},{3,1},{4,6},{5,7},{6,4},{7,5},{8,10},{9,11},{10,... | collective-permute-start | bytes 122888 | tf_op jit(solution)/shard_map/ppermute | solution.py:65
  158.0 10.3 %collective-permute-start.2 = (bf16[4,320,32]{1,2,0:T(8,128)(2,1)S(1)}, bf16[4,320,32]{1,2,0:T(8,128)(2,1)S(1)}, u32[]{:S(2)}, u32[]{:S(2)}) collective-permute-start(bf16[4,320,32]{1,2,0:T(8,128)(2,1)S(1)} %maximum_select_fusion.1), channel_id=1, source_target_pairs={{0,4},{1,5},{2,6},{3,7},{4,0},{5,1},{6,2},{7,3},{8,12},{9,13},{10,... | collective-permute-start | bytes 245768 | tf_op jit(solution)/shard_map/ppermute | solution.py:65
  171.7 4.2 %all-to-all-start.5 = ((bf16[4,1,320,128]{3,2,1,0:T(8,128)(2,1)}), bf16[4,1,320,128]{3,2,1,0:T(8,128)(2,1)S(1)}, u32[]{:S(2)}, u32[]{:S(2)}) async-start(bf16[4,1,320,128]{3,2,1,0:T(8,128)(2,1)} %broadcast_in_dim.28), calls=%async_computation.5 | async-start | bytes 655360 | tf_op jit(solution)/shard_map/all_to_all | solution.py:53
  177.8 4.3 %copy.189 = bf16[16,128,4,128]{3,2,1,0:T(4,128)(2,1)} copy(bf16[16,128,4,128]{1,3,0,2:T(8,128)(2,1)} %fusion.6) | data formatting | bytes 4194304 | tf_op jit(solution)/shard_map/transpose | solution.py:112
  182.0 5.5 %all-to-all-start.7 = ((bf16[16,128,4,128]{3,2,1,0:T(4,128)(2,1)}), bf16[16,128,4,128]{3,2,1,0:T(4,128)(2,1)S(1)}, u32[]{:S(2)}, u32[]{:S(2)}) async-start(bf16[16,128,4,128]{3,2,1,0:T(4,128)(2,1)} %copy.189), calls=%async_computation.7 | async-start | bytes 4194304 | tf_op jit(solution)/shard_map/all_to_all | solution.py:113
  187.8 39.6 %all-to-all-done.7 = bf16[16,128,4,128]{3,2,1,0:T(4,128)(2,1)S(1)} async-done(((bf16[16,128,4,128]{3,2,1,0:T(4,128)(2,1)}), bf16[16,128,4,128]{3,2,1,0:T(4,128)(2,1)S(1)}, u32[]{:S(2)}, u32[]{:S(2)}) %all-to-all-start.7) | async-done | bytes 2097184 | tf_op jit(solution)/shard_map/all_to_all | solution.py:113
  228.8 11.0 %all-to-all-start.6 = ((bf16[4,4,320,128]{3,1,2,0:T(4,128)(2,1)}), bf16[4,4,320,128]{3,1,2,0:T(4,128)(2,1)S(1)}, u32[]{:S(2)}, u32[]{:S(2)}) async-start(bf16[4,4,320,128]{3,1,2,0:T(4,128)(2,1)} %broadcast_in_dim.30), calls=%async_computation.6 | async-start | bytes 2621440 | tf_op jit(solution)/shard_map/all_to_all | solution.py:53
  241.6 3.9 %copy.190 = bf16[2048,512]{0,1:T(8,128)(2,1)} copy(bf16[2048,512]{1,0:T(8,128)(2,1)} %bitcast.95) | data formatting | bytes 4194304 | tf_op jit(solution)/shard_map/reshape | solution.py:114
  245.5 25.3 %all-to-all-done.6 = bf16[4,4,320,128]{3,1,2,0:T(4,128)(2,1)S(1)} async-done(((bf16[4,4,320,128]{3,1,2,0:T(4,128)(2,1)}), bf16[4,4,320,128]{3,1,2,0:T(4,128)(2,1)S(1)}, u32[]{:S(2)}, u32[]{:S(2)}) %all-to-all-start.6) | async-done | bytes 1310752 | tf_op jit(solution)/shard_map/all_to_all | solution.py:53
  275.6 11.8 %all_to_all.46 = f32[4,320,128]{2,1,0:T(8,128)S(1)} all-to-all(f32[4,320,128]{2,1,0:T(8,128)S(1)} %convolution_bitcast_fusion), channel_id=1, replica_groups=mesh['section'=8,'tp_x'=4,'tp_z'=4,'tp_y'=4] {'tp_x'}, dimensions={0} | all-to-all | bytes 1310720 | tf_op jit(solution)/shard_map/all_to_all | solution.py:158
  287.5 11.2 %collective-permute-start.3 = (bf16[320,128]{1,0:T(8,128)(2,1)S(1)}, bf16[320,128]{1,0:T(8,128)(2,1)S(1)}, u32[]{:S(2)}, u32[]{:S(2)}) collective-permute-start(bf16[320,128]{1,0:T(8,128)(2,1)S(1)} %add_convert_fusion), channel_id=1, source_target_pairs={{0,64},{64,128},{128,192},{192,256},{256,320},{320,384},{384,448},... | collective-permute-start | bytes 245768 | tf_op jit(solution)/shard_map/ppermute | solution.py:21
  (98 shorter events, 40.3 us)
Async XLA Ops:
  11.8 7.8 %copy-start.4 = (f32[1,1,64]{2,1,0:T(1,128)S(1)}, f32[1,1,64]{2,1,0:T(1,128)}, u32[]{:S(2)}) copy-start(f32[1,1,64]{2,1,0:T(1,128)} %param.21) | copy-start | bytes 772
  11.8 7.8 %copy-start.5 = (s32[1,1,64]{2,1,0:T(1,128)S(1)}, s32[1,1,64]{2,1,0:T(1,128)}, u32[]{:S(2)}) copy-start(s32[1,1,64]{2,1,0:T(1,128)} %param.22) | copy-start | bytes 772
  11.8 7.8 %copy-start.6 = (f32[1,1,64]{2,1,0:T(1,128)S(1)}, f32[1,1,64]{2,1,0:T(1,128)}, u32[]{:S(2)}) copy-start(f32[1,1,64]{2,1,0:T(1,128)} %param.15) | copy-start | bytes 772
  11.9 7.8 %copy-start.7 = (s32[1,1,64]{2,1,0:T(1,128)S(1)}, s32[1,1,64]{2,1,0:T(1,128)}, u32[]{:S(2)}) copy-start(s32[1,1,64]{2,1,0:T(1,128)} %param.16) | copy-start | bytes 772
  11.9 7.9 %copy-start.9 = (f32[1,1,16]{2,1,0:T(1,128)S(1)}, f32[1,1,16]{2,1,0:T(1,128)}, u32[]{:S(2)}) copy-start(f32[1,1,16]{2,1,0:T(1,128)} %param.18) | copy-start | bytes 196
  11.9 7.9 %copy-start.10 = (s32[1,1,16]{2,1,0:T(1,128)S(1)}, s32[1,1,16]{2,1,0:T(1,128)}, u32[]{:S(2)}) copy-start(s32[1,1,16]{2,1,0:T(1,128)} %param.19) | copy-start | bytes 196
  11.9 8.0 %copy-start.2 = (bf16[1,128,2048]{2,1,0:T(8,128)(2,1)S(1)}, bf16[1,128,2048]{2,1,0:T(8,128)(2,1)}, u32[]{:S(2)}) copy-start(bf16[1,128,2048]{2,1,0:T(8,128)(2,1)} %param.17) | copy-start | bytes 1572868
  13.3 37.4 %all-to-all-start.1 = ((bf16[4,4,321,128]{3,1,2,0:T(4,128)(2,1)}), bf16[4,4,321,128]{3,1,2,0:T(4,128)(2,1)}, u32[]{:S(2)}, u32[]{:S(2)}) async-start(bf16[4,4,321,128]{3,1,2,0:T(4,128)(2,1)} %broadcast_in_dim.23), calls=%async_computation.1 | async-start | bytes 2629632 | tf_op jit(solution)/shard_map/all_to_all | solution.py:53
  53.1 8.2 %all-to-all-start.2 = ((f32[4,1,320]{2,1,0:T(1,128)}), f32[4,1,320]{2,1,0:T(1,128)S(1)}, u32[]{:S(2)}, u32[]{:S(2)}) async-start(f32[4,1,320]{2,1,0:T(1,128)} %broadcast_in_dim.24), calls=%async_computation.2 | async-start | bytes 12288 | tf_op jit(solution)/shard_map/all_to_all | solution.py:53
  61.3 55.1 %all-to-all-start.3 = ((bf16[16,128,640]{1,2,0:T(8,128)(2,1)}), bf16[16,128,640]{1,2,0:T(8,128)(2,1)}, u32[]{:S(2)}, u32[]{:S(2)}) async-start(bf16[16,128,640]{1,2,0:T(8,128)(2,1)} %pad_maximum_fusion), calls=%async_computation.3 | async-start | bytes 5242880 | tf_op jit(solution)/shard_map/all_to_all | solution.py:108
  124.2 2.3 copy-start.1
  128.9 15.0 %all-to-all-start.4 = ((f32[4,320,160]{1,2,0:T(8,128)}), f32[4,320,160]{1,2,0:T(8,128)S(1)}, u32[]{:S(2)}, u32[]{:S(2)}) async-start(f32[4,320,160]{1,2,0:T(8,128)} %copy.174), calls=%async_computation.4 | async-start | bytes 1966080 | tf_op jit(solution)/shard_map/all_to_all | solution.py:132
  144.0 26.4 %copy-start.8 = (s32[320]{0:T(512)S(1)}, s32[320]{0:T(512)}, u32[]{:S(2)}) copy-start(s32[320]{0:T(512)} %param.23) | copy-start | bytes 3844
  144.6 4.6 %collective-permute-start = (bf16[1,320,32]{1,2,0:T(8,128)(2,1)S(1)}, bf16[1,320,32]{1,2,0:T(8,128)(2,1)S(1)}, u32[]{:S(2)}, u32[]{:S(2)}) collective-permute-start(bf16[1,320,32]{1,2,0:T(8,128)(2,1)S(1)} %pad_maximum_fusion.3), channel_id=1, source_target_pairs={{0,1},{1,0},{2,3},{3,2},{4,5},{5,4},{6,7},{7,6},{8,9},{9,8},{10,11... | collective-permute-start | bytes 61448 | tf_op jit(solution)/shard_map/ppermute | solution.py:65
  149.2 8.8 %collective-permute-start.1 = (bf16[2,320,32]{1,2,0:T(8,128)(2,1)S(1)}, bf16[2,320,32]{1,2,0:T(8,128)(2,1)S(1)}, u32[]{:S(2)}, u32[]{:S(2)}) collective-permute-start(bf16[2,320,32]{1,2,0:T(8,128)(2,1)S(1)} %maximum_select_fusion.2), channel_id=1, source_target_pairs={{0,2},{1,3},{2,0},{3,1},{4,6},{5,7},{6,4},{7,5},{8,10},{9,11},{10,... | collective-permute-start | bytes 122888 | tf_op jit(solution)/shard_map/ppermute | solution.py:65
  158.0 12.3 %collective-permute-start.2 = (bf16[4,320,32]{1,2,0:T(8,128)(2,1)S(1)}, bf16[4,320,32]{1,2,0:T(8,128)(2,1)S(1)}, u32[]{:S(2)}, u32[]{:S(2)}) collective-permute-start(bf16[4,320,32]{1,2,0:T(8,128)(2,1)S(1)} %maximum_select_fusion.1), channel_id=1, source_target_pairs={{0,4},{1,5},{2,6},{3,7},{4,0},{5,1},{6,2},{7,3},{8,12},{9,13},{10,... | collective-permute-start | bytes 245768 | tf_op jit(solution)/shard_map/ppermute | solution.py:65
  171.7 10.3 %all-to-all-start.5 = ((bf16[4,1,320,128]{3,2,1,0:T(8,128)(2,1)}), bf16[4,1,320,128]{3,2,1,0:T(8,128)(2,1)S(1)}, u32[]{:S(2)}, u32[]{:S(2)}) async-start(bf16[4,1,320,128]{3,2,1,0:T(8,128)(2,1)} %broadcast_in_dim.28), calls=%async_computation.5 | async-start | bytes 655360 | tf_op jit(solution)/shard_map/all_to_all | solution.py:53
  182.0 45.4 %all-to-all-start.7 = ((bf16[16,128,4,128]{3,2,1,0:T(4,128)(2,1)}), bf16[16,128,4,128]{3,2,1,0:T(4,128)(2,1)S(1)}, u32[]{:S(2)}, u32[]{:S(2)}) async-start(bf16[16,128,4,128]{3,2,1,0:T(4,128)(2,1)} %copy.189), calls=%async_computation.7 | async-start | bytes 4194304 | tf_op jit(solution)/shard_map/all_to_all | solution.py:113
  228.8 42.0 %all-to-all-start.6 = ((bf16[4,4,320,128]{3,1,2,0:T(4,128)(2,1)}), bf16[4,4,320,128]{3,1,2,0:T(4,128)(2,1)S(1)}, u32[]{:S(2)}, u32[]{:S(2)}) async-start(bf16[4,4,320,128]{3,1,2,0:T(4,128)(2,1)} %broadcast_in_dim.30), calls=%async_computation.6 | async-start | bytes 2621440 | tf_op jit(solution)/shard_map/all_to_all | solution.py:53
  271.1 2.3 copy-start
  275.6 11.9 %copy-start.3 = (bf16[1,320,128]{2,1,0:T(8,128)(2,1)S(1)}, bf16[1,320,128]{2,1,0:T(8,128)(2,1)}, u32[]{:S(2)}) copy-start(bf16[1,320,128]{2,1,0:T(8,128)(2,1)} %param.12) | copy-start | bytes 245764
  287.5 12.7 %collective-permute-start.3 = (bf16[320,128]{1,0:T(8,128)(2,1)S(1)}, bf16[320,128]{1,0:T(8,128)(2,1)S(1)}, u32[]{:S(2)}, u32[]{:S(2)}) collective-permute-start(bf16[320,128]{1,0:T(8,128)(2,1)S(1)} %add_convert_fusion), channel_id=1, source_target_pairs={{0,64},{64,128},{128,192},{192,256},{256,320},{320,384},{384,448},... | collective-permute-start | bytes 245768 | tf_op jit(solution)/shard_map/ppermute | solution.py:21

commit v6 on v5

--- a/solution.py
+++ b/solution.py
@@ -104,14 +104,14 @@
     kv_eff = dequant(kv_weight[0], kv_scale[0], kv_keep[0])
     kv_send = kv_eff.reshape(own_width, 2, planes, halves, members, chunk)
     kv_send = kv_send.transpose(3, 4, 0, 2, 1, 5).reshape(plane, own_width, planes * 2 * chunk)
-    both = jnp.concatenate([q_send, kv_send], axis=2)
+    o_eff = dequant(out_weight[0], out_scale[0], out_keep[0])
+    o_send = o_eff.reshape(q_width, planes, plane, own_width).transpose(2, 0, 1, 3)
+    o_send = o_send.reshape(plane, q_width, planes * own_width)
+    both = jnp.concatenate([q_send, kv_send, o_send], axis=2)
     both = lax.all_to_all(both, PLANE, 0, 0, tiled=True).reshape(plane * own_width, -1)
     q_rows = both[:, : planes * q_width]
-    kv_rows = both[:, planes * q_width :]
-    o_eff = dequant(out_weight[0], out_scale[0], out_keep[0])
-    o_send = o_eff.reshape(q_width, planes, plane, own_width).transpose(2, 0, 1, 3)
-    o_rows = lax.all_to_all(o_send, PLANE, 0, 0, tiled=True)
-    o_rows = o_rows.reshape(plane * q_width, planes * own_width)
+    kv_rows = both[:, planes * q_width : planes * (q_width + 2 * chunk)]
+    o_rows = both[:, planes * (q_width + 2 * chunk) :]
 
     extended = jnp.concatenate([local_rows, norm_gain[0][None]], axis=0)
     gathered = gather_all(extended, PLANE)

time: 302 us -> 300 us (level)
  blocking collectives: 22.6 us -> 30.8 us
  waiting for transfers between devices: 154 us -> 147 us
  starting transfers between devices: 69.9 us -> 64.5 us
  local copies, waits for them, and re-layouts: 39.6 us -> 43.2 us
    all_to_all x1 -> x0, waiting for transfers between devices: 39.6 us -> none  [local(): o_rows = lax.all_to_all(o_send, PLANE, 0, 0, tiled=True)]
    all_to_all x1, waiting for transfers between devices: 47.8 us -> 84.5 us  [local(): lax.all_to_all(both, PLANE, 0, 0, tiled=True).reshape(plane * own_width, -1)]
    all_to_all x4 -> x3, starting transfers between devices: 25.6 us -> 13.8 us  [gather_all(): held = lax.all_to_all(spread, axis, 0, 0, tiled=True)]
    all_to_all x1 -> x2, blocking collectives: 10.7 us -> 20.6 us  [gather_all(): held = lax.all_to_all(spread, axis, 0, 0, tiled=True)]
    ppermute x3, starting transfers between devices: 19.6 us -> 27.8 us  [group_gather(): other = lax.ppermute(held, axis, pairs)]
    all_to_all x4 -> x3, waiting for transfers between devices: 52.3 us -> 44.6 us  [gather_all(): held = lax.all_to_all(spread, axis, 0, 0, tiled=True)]
    dot_general x0 -> x2, local copies, waits for them, and re-layouts: none -> 6.36 us  [local(): out_part = jnp.dot(heads_pl, o_rows, preferred_element_type=jnp.float32)]
    all_to_all x1 -> x0, starting transfers between devices: 5.53 us -> none  [local(): o_rows = lax.all_to_all(o_send, PLANE, 0, 0, tiled=True)]
  transfers between devices with their start and end apart: 11 -> 9, of which waited for: 10 -> 9; matrix products, arithmetic and copies ran while one was open for 9% -> 7% of each run, Pallas kernels for 0% -> 0%
where the time goes in v6:
time: 300 us; the launch traced here: 299 us
  waiting for transfers between devices  147 us (49%)
  starting transfers between devices  64.5 us (22%)
  local copies, waits for them, and re-layouts  43.2 us (14%)
  blocking collectives  30.8 us (10%)
  other arithmetic  7.49 us (2%)
  matrix products  5.75 us (2%)
    all_to_all x1, waiting for transfers between devices, local(): lax.all_to_all(both, PLANE, 0, 0, tiled=True).reshape(plane * own_width, -1)  84.5 us
    all_to_all x3, waiting for transfers between devices, gather_all(): held = lax.all_to_all(spread, axis, 0, 0, tiled=True)  44.6 us
    ppermute x3, starting transfers between devices, group_gather(): other = lax.ppermute(held, axis, pairs)  27.8 us
    all_to_all x2, blocking collectives, gather_all(): held = lax.all_to_all(spread, axis, 0, 0, tiled=True)  20.6 us
    ppermute x1, starting transfers between devices, passed_along(): return lax.ppermute(value, axis, pairs)  14.6 us
    all_to_all x3, starting transfers between devices, gather_all(): held = lax.all_to_all(spread, axis, 0, 0, tiled=True)  13.8 us
    all_to_all x1, waiting for transfers between devices, local(): summed = jnp.sum(lax.all_to_all(packed, CROSS, 0, 0, tiled=True), axis=0)  11.4 us
    all_to_all x1, blocking collectives, local(): lax.all_to_all(out_part, CROSS, 0, 0, tiled=True)  10.2 us
  transfers between devices with their start and end apart: 9, of which 9 were waited for; matrix products, arithmetic and copies ran while one was open for 7% of the time, Pallas kernels for 0%

profile of v6, /device:TPU:1, one launch (start us, length us, event | category | flops | bytes accessed | tf_op | source)
XLA Modules:
  0.0 299.1 jit_solution(14588012790392311283)
XLA Ops:
  1.0 10.7 %all_to_all.40 = bf16[4,1,321,128]{3,2,1,0:T(8,128)(2,1)S(1)} all-to-all(bf16[4,1,321,128]{3,2,1,0:T(8,128)(2,1)S(1)} %broadcast_in_dim.21), channel_id=1, replica_groups=mesh['section'=8,'tp_x'=4,'tp_z'=4,'tp_y'=4] {'tp_y'}, dimensions={0} | all-to-all | bytes 657408 | tf_op jit(solution)/shard_map/all_to_all | solution.py:53
  13.3 6.3 %all-to-all-start.1 = ((bf16[4,4,321,128]{3,1,2,0:T(4,128)(2,1)}), bf16[4,4,321,128]{3,1,2,0:T(4,128)(2,1)}, u32[]{:S(2)}, u32[]{:S(2)}) async-start(bf16[4,4,321,128]{3,1,2,0:T(4,128)(2,1)} %broadcast_in_dim.23), calls=%async_computation.1 | async-start | bytes 2629632 | tf_op jit(solution)/shard_map/all_to_all | solution.py:53
  21.3 3.2 %copy.168 = bf16[1,128,8192]{1,2,0:T(8,128)(2,1)S(1)} copy(bf16[1,128,8192]{2,1,0:T(8,128)(2,1)} %param.14) | data formatting | bytes 4194304 | tf_op args[2]
  26.5 3.2 %copy.172 = bf16[1,128,8192]{1,2,0:T(8,128)(2,1)S(1)} copy(bf16[1,128,8192]{2,1,0:T(8,128)(2,1)} %param.20) | data formatting | bytes 4194304 | tf_op args[8]
  31.7 19.0 %all-to-all-done.1 = bf16[4,4,321,128]{3,1,2,0:T(4,128)(2,1)} async-done(((bf16[4,4,321,128]{3,1,2,0:T(4,128)(2,1)}), bf16[4,4,321,128]{3,1,2,0:T(4,128)(2,1)}, u32[]{:S(2)}, u32[]{:S(2)}) %all-to-all-start.1) | async-done | bytes 1314848 | tf_op jit(solution)/shard_map/all_to_all | solution.py:53
  53.2 4.0 %all-to-all-start.2 = ((f32[4,1,320]{2,1,0:T(1,128)}), f32[4,1,320]{2,1,0:T(1,128)S(1)}, u32[]{:S(2)}, u32[]{:S(2)}) async-start(f32[4,1,320]{2,1,0:T(1,128)} %broadcast_in_dim.24), calls=%async_computation.2 | async-start | bytes 12288 | tf_op jit(solution)/shard_map/all_to_all | solution.py:53
  57.2 3.6 %pad_maximum_fusion = bf16[16,128,1152]{1,2,0:T(8,128)(2,1)} fusion(bf16[16,128,512]{1,2,0:T(8,128)(2,1)} %bitcast.90, bf16[16,128,128]{1,2,0:T(8,128)(2,1)} %bitcast.92, bf16[16,128,512]{1,2,0:T(8,128)(2,1)S(1)} %bitcast.89), kind=kLoop, calls=%fused_computation | loop fusion | flops 14155776 | bytes 9437184 | tf_op jit(solution)/shard_map/concatenate | solution.py:110
  61.3 4.6 %all-to-all-start.3 = ((bf16[16,128,1152]{1,2,0:T(8,128)(2,1)}), bf16[16,128,1152]{1,2,0:T(8,128)(2,1)}, u32[]{:S(2)}, u32[]{:S(2)}) async-start(bf16[16,128,1152]{1,2,0:T(8,128)(2,1)} %pad_maximum_fusion), calls=%async_computation.3 | async-start | bytes 9437184 | tf_op jit(solution)/shard_map/all_to_all | solution.py:111
  68.8 84.5 %all-to-all-done.3 = bf16[16,128,1152]{1,2,0:T(8,128)(2,1)} async-done(((bf16[16,128,1152]{1,2,0:T(8,128)(2,1)}), bf16[16,128,1152]{1,2,0:T(8,128)(2,1)}, u32[]{:S(2)}, u32[]{:S(2)}) %all-to-all-start.3) | async-done | bytes 4718624 | tf_op jit(solution)/shard_map/all_to_all | solution.py:111
  153.2 6.7 %copy.174 = bf16[16,128,1152]{2,1,0:T(8,128)(2,1)} copy(bf16[16,128,1152]{1,2,0:T(8,128)(2,1)} %all-to-all-done.3) | data formatting | bytes 9437184 | tf_op jit(solution)/shard_map/all_to_all | solution.py:111
  161.0 3.9 %slice_bitcast_fusion = (bf16[512,2048]{0,1:T(8,128)(2,1)S(1)}, bf16[512,2048]{0,1:T(8,128)(2,1)}) fusion(bf16[2048,1152]{1,0:T(8,128)(2,1)} %bitcast.83), kind=kLoop, calls=%fused_computation.12 | loop fusion | bytes 8388608 | tf_op jit(solution)/shard_map/dot_general | solution.py:156
  165.9 4.1 %copy.175 = bf16[512,2048]{1,0:T(8,128)(2,1)} copy(bf16[512,2048]{0,1:T(8,128)(2,1)} %get-tuple-element.6) | data formatting | bytes 4194304 | tf_op jit(solution)/shard_map/dot_general | solution.py:126
  174.5 3.7 %all-to-all-start.4 = ((f32[4,320,160]{1,2,0:T(8,128)}), f32[4,320,160]{1,2,0:T(8,128)S(1)}, u32[]{:S(2)}, u32[]{:S(2)}) async-start(f32[4,320,160]{1,2,0:T(8,128)} %copy.178), calls=%async_computation.4 | async-start | bytes 1966080 | tf_op jit(solution)/shard_map/all_to_all | solution.py:132
  178.2 11.4 %all-to-all-done.4 = f32[4,320,160]{1,2,0:T(8,128)S(1)} async-done(((f32[4,320,160]{1,2,0:T(8,128)}), f32[4,320,160]{1,2,0:T(8,128)S(1)}, u32[]{:S(2)}, u32[]{:S(2)}) %all-to-all-start.4) | async-done | bytes 819232 | tf_op jit(solution)/shard_map/all_to_all | solution.py:132
  190.3 2.2 collective-permute-start
  192.7 2.2 collective-permute-done
  194.9 9.5 %collective-permute-start.1 = (bf16[2,320,32]{1,2,0:T(8,128)(2,1)S(1)}, bf16[2,320,32]{1,2,0:T(8,128)(2,1)S(1)}, u32[]{:S(2)}, u32[]{:S(2)}) collective-permute-start(bf16[2,320,32]{1,2,0:T(8,128)(2,1)S(1)} %maximum_select_fusion.2), channel_id=1, source_target_pairs={{0,2},{1,3},{2,0},{3,1},{4,6},{5,7},{6,4},{7,5},{8,10},{9,11},{10,... | collective-permute-start | bytes 122888 | tf_op jit(solution)/shard_map/ppermute | solution.py:65
  205.9 16.1 %collective-permute-start.2 = (bf16[4,320,32]{1,2,0:T(8,128)(2,1)S(1)}, bf16[4,320,32]{1,2,0:T(8,128)(2,1)S(1)}, u32[]{:S(2)}, u32[]{:S(2)}) collective-permute-start(bf16[4,320,32]{1,2,0:T(8,128)(2,1)S(1)} %maximum_select_fusion.1), channel_id=1, source_target_pairs={{0,4},{1,5},{2,6},{3,7},{4,0},{5,1},{6,2},{7,3},{8,12},{9,13},{10,... | collective-permute-start | bytes 245768 | tf_op jit(solution)/shard_map/ppermute | solution.py:65
  224.8 9.9 %all_to_all.41 = bf16[4,1,320,128]{3,2,1,0:T(8,128)(2,1)S(1)} all-to-all(bf16[4,1,320,128]{3,2,1,0:T(8,128)(2,1)S(1)} %broadcast_in_dim.28), channel_id=1, replica_groups=mesh['section'=8,'tp_x'=4,'tp_z'=4,'tp_y'=4] {'tp_y'}, dimensions={0} | all-to-all | bytes 655360 | tf_op jit(solution)/shard_map/all_to_all | solution.py:53
  236.3 3.5 %all-to-all-start.6 = ((bf16[4,4,320,128]{3,1,2,0:T(4,128)(2,1)}), bf16[4,4,320,128]{3,1,2,0:T(4,128)(2,1)S(1)}, u32[]{:S(2)}, u32[]{:S(2)}) async-start(bf16[4,4,320,128]{3,1,2,0:T(4,128)(2,1)} %broadcast_in_dim.30), calls=%async_computation.6 | async-start | bytes 2621440 | tf_op jit(solution)/shard_map/all_to_all | solution.py:53
  239.9 2.5 copy.192
  242.3 25.0 %all-to-all-done.6 = bf16[4,4,320,128]{3,1,2,0:T(4,128)(2,1)S(1)} async-done(((bf16[4,4,320,128]{3,1,2,0:T(4,128)(2,1)}), bf16[4,4,320,128]{3,1,2,0:T(4,128)(2,1)S(1)}, u32[]{:S(2)}, u32[]{:S(2)}) %all-to-all-start.6) | async-done | bytes 1310752 | tf_op jit(solution)/shard_map/all_to_all | solution.py:53
  272.1 10.2 %all_to_all.42 = f32[4,320,128]{2,1,0:T(8,128)S(1)} all-to-all(f32[4,320,128]{2,1,0:T(8,128)S(1)} %convolution_bitcast_fusion), channel_id=1, replica_groups=mesh['section'=8,'tp_x'=4,'tp_z'=4,'tp_y'=4] {'tp_x'}, dimensions={0} | all-to-all | bytes 1310720 | tf_op jit(solution)/shard_map/all_to_all | solution.py:158
  282.4 14.6 %collective-permute-start.3 = (bf16[320,128]{1,0:T(8,128)(2,1)S(1)}, bf16[320,128]{1,0:T(8,128)(2,1)S(1)}, u32[]{:S(2)}, u32[]{:S(2)}) collective-permute-start(bf16[320,128]{1,0:T(8,128)(2,1)S(1)} %add_convert_fusion), channel_id=1, source_target_pairs={{0,64},{64,128},{128,192},{192,256},{256,320},{320,384},{384,448},... | collective-permute-start | bytes 245768 | tf_op jit(solution)/shard_map/ppermute | solution.py:21
  (98 shorter events, 34.1 us)
Async XLA Ops:
  11.8 7.8 %copy-start.6 = (f32[1,1,64]{2,1,0:T(1,128)S(1)}, f32[1,1,64]{2,1,0:T(1,128)}, u32[]{:S(2)}) copy-start(f32[1,1,64]{2,1,0:T(1,128)} %param.21) | copy-start | bytes 772
  11.8 7.8 %copy-start.7 = (s32[1,1,64]{2,1,0:T(1,128)S(1)}, s32[1,1,64]{2,1,0:T(1,128)}, u32[]{:S(2)}) copy-start(s32[1,1,64]{2,1,0:T(1,128)} %param.22) | copy-start | bytes 772
  11.8 7.8 %copy-start.8 = (f32[1,1,64]{2,1,0:T(1,128)S(1)}, f32[1,1,64]{2,1,0:T(1,128)}, u32[]{:S(2)}) copy-start(f32[1,1,64]{2,1,0:T(1,128)} %param.15) | copy-start | bytes 772
  11.9 7.8 %copy-start.9 = (s32[1,1,64]{2,1,0:T(1,128)S(1)}, s32[1,1,64]{2,1,0:T(1,128)}, u32[]{:S(2)}) copy-start(s32[1,1,64]{2,1,0:T(1,128)} %param.16) | copy-start | bytes 772
  11.9 8.0 %copy-start.11 = (f32[1,1,16]{2,1,0:T(1,128)S(1)}, f32[1,1,16]{2,1,0:T(1,128)}, u32[]{:S(2)}) copy-start(f32[1,1,16]{2,1,0:T(1,128)} %param.18) | copy-start | bytes 196
  11.9 7.9 %copy-start.12 = (s32[1,1,16]{2,1,0:T(1,128)S(1)}, s32[1,1,16]{2,1,0:T(1,128)}, u32[]{:S(2)}) copy-start(s32[1,1,16]{2,1,0:T(1,128)} %param.19) | copy-start | bytes 196
  11.9 8.0 %copy-start.4 = (bf16[1,128,2048]{2,1,0:T(8,128)(2,1)S(1)}, bf16[1,128,2048]{2,1,0:T(8,128)(2,1)}, u32[]{:S(2)}) copy-start(bf16[1,128,2048]{2,1,0:T(8,128)(2,1)} %param.17) | copy-start | bytes 1572868
  13.3 37.4 %all-to-all-start.1 = ((bf16[4,4,321,128]{3,1,2,0:T(4,128)(2,1)}), bf16[4,4,321,128]{3,1,2,0:T(4,128)(2,1)}, u32[]{:S(2)}, u32[]{:S(2)}) async-start(bf16[4,4,321,128]{3,1,2,0:T(4,128)(2,1)} %broadcast_in_dim.23), calls=%async_computation.1 | async-start | bytes 2629632 | tf_op jit(solution)/shard_map/all_to_all | solution.py:53
  31.7 25.5 %copy-start = (bf16[16,128,4,128]{1,3,2,0:T(8,128)(2,1)S(1)}, bf16[16,128,4,128]{1,3,2,0:T(8,128)(2,1)}, u32[]{:S(2)}) copy-start(bf16[16,128,4,128]{1,3,2,0:T(8,128)(2,1)} %copy.169) | copy-start | bytes 6291460
  53.2 8.2 %all-to-all-start.2 = ((f32[4,1,320]{2,1,0:T(1,128)}), f32[4,1,320]{2,1,0:T(1,128)S(1)}, u32[]{:S(2)}, u32[]{:S(2)}) async-start(f32[4,1,320]{2,1,0:T(1,128)} %broadcast_in_dim.24), calls=%async_computation.2 | async-start | bytes 12288 | tf_op jit(solution)/shard_map/all_to_all | solution.py:53
  61.3 91.9 %all-to-all-start.3 = ((bf16[16,128,1152]{1,2,0:T(8,128)(2,1)}), bf16[16,128,1152]{1,2,0:T(8,128)(2,1)}, u32[]{:S(2)}, u32[]{:S(2)}) async-start(bf16[16,128,1152]{1,2,0:T(8,128)(2,1)} %pad_maximum_fusion), calls=%async_computation.3 | async-start | bytes 9437184 | tf_op jit(solution)/shard_map/all_to_all | solution.py:111
  165.9 4.1 %copy-start.3 = (bf16[320,2048,1]{1,0,2:T(8,128)(2,1)S(1)}, bf16[320,2048,1]{1,0,2:T(8,128)(2,1)}, u32[]{:S(2)}) copy-start(bf16[320,2048,1]{1,0,2:T(8,128)(2,1)} %reshape.482) | copy-start | bytes 3932164
  170.0 2.0 copy-start.2
  174.5 15.1 %all-to-all-start.4 = ((f32[4,320,160]{1,2,0:T(8,128)}), f32[4,320,160]{1,2,0:T(8,128)S(1)}, u32[]{:S(2)}, u32[]{:S(2)}) async-start(f32[4,320,160]{1,2,0:T(8,128)} %copy.178), calls=%async_computation.4 | async-start | bytes 1966080 | tf_op jit(solution)/shard_map/all_to_all | solution.py:132
  189.6 34.4 %copy-start.10 = (s32[320]{0:T(512)S(1)}, s32[320]{0:T(512)}, u32[]{:S(2)}) copy-start(s32[320]{0:T(512)} %param.23) | copy-start | bytes 3844
  190.3 4.6 %collective-permute-start = (bf16[1,320,32]{1,2,0:T(8,128)(2,1)S(1)}, bf16[1,320,32]{1,2,0:T(8,128)(2,1)S(1)}, u32[]{:S(2)}, u32[]{:S(2)}) collective-permute-start(bf16[1,320,32]{1,2,0:T(8,128)(2,1)S(1)} %pad_maximum_fusion.3), channel_id=1, source_target_pairs={{0,1},{1,0},{2,3},{3,2},{4,5},{5,4},{6,7},{7,6},{8,9},{9,8},{10,11... | collective-permute-start | bytes 61448 | tf_op jit(solution)/shard_map/ppermute | solution.py:65
  194.9 10.9 %collective-permute-start.1 = (bf16[2,320,32]{1,2,0:T(8,128)(2,1)S(1)}, bf16[2,320,32]{1,2,0:T(8,128)(2,1)S(1)}, u32[]{:S(2)}, u32[]{:S(2)}) collective-permute-start(bf16[2,320,32]{1,2,0:T(8,128)(2,1)S(1)} %maximum_select_fusion.2), channel_id=1, source_target_pairs={{0,2},{1,3},{2,0},{3,1},{4,6},{5,7},{6,4},{7,5},{8,10},{9,11},{10,... | collective-permute-start | bytes 122888 | tf_op jit(solution)/shard_map/ppermute | solution.py:65
  205.9 18.1 %collective-permute-start.2 = (bf16[4,320,32]{1,2,0:T(8,128)(2,1)S(1)}, bf16[4,320,32]{1,2,0:T(8,128)(2,1)S(1)}, u32[]{:S(2)}, u32[]{:S(2)}) collective-permute-start(bf16[4,320,32]{1,2,0:T(8,128)(2,1)S(1)} %maximum_select_fusion.1), channel_id=1, source_target_pairs={{0,4},{1,5},{2,6},{3,7},{4,0},{5,1},{6,2},{7,3},{8,12},{9,13},{10,... | collective-permute-start | bytes 245768 | tf_op jit(solution)/shard_map/ppermute | solution.py:65
  236.3 31.0 %all-to-all-start.6 = ((bf16[4,4,320,128]{3,1,2,0:T(4,128)(2,1)}), bf16[4,4,320,128]{3,1,2,0:T(4,128)(2,1)S(1)}, u32[]{:S(2)}, u32[]{:S(2)}) async-start(bf16[4,4,320,128]{3,1,2,0:T(4,128)(2,1)} %broadcast_in_dim.30), calls=%async_computation.6 | async-start | bytes 2621440 | tf_op jit(solution)/shard_map/all_to_all | solution.py:53
  267.6 2.3 copy-start.1
  272.1 10.2 %copy-start.5 = (bf16[1,320,128]{2,1,0:T(8,128)(2,1)S(1)}, bf16[1,320,128]{2,1,0:T(8,128)(2,1)}, u32[]{:S(2)}) copy-start(bf16[1,320,128]{2,1,0:T(8,128)(2,1)} %param.12) | copy-start | bytes 245764
  282.4 16.1 %collective-permute-start.3 = (bf16[320,128]{1,0:T(8,128)(2,1)S(1)}, bf16[320,128]{1,0:T(8,128)(2,1)S(1)}, u32[]{:S(2)}, u32[]{:S(2)}) collective-permute-start(bf16[320,128]{1,0:T(8,128)(2,1)S(1)} %add_convert_fusion), channel_id=1, source_target_pairs={{0,64},{64,128},{128,192},{192,256},{256,320},{320,384},{384,448},... | collective-permute-start | bytes 245768 | tf_op jit(solution)/shard_map/ppermute | solution.py:21
